TPU v7x, 256 devices: a whole 4x4x8 slice. The times are simulated.
256 devices in a mesh: row: 8 (over x, core), col: 32 (over z, y).
Axes of the slice: x: 4, y: 4, z: 8, core: 2. Of those that a mesh axis runs over, the one named last changes fastest.
Arguments:
- row_points: bfloat16 [512, 64, 256], P('row'), may hold values from -25.5 to 25.5
- col_points: bfloat16 [128, 64, 256], P('col'), may hold values from -25.5 to 25.5
- block_lists: int32 [512, 16], P('row'), may hold values from 0 to 127, as said below
Outputs:
- row_potential: float32 [512, 256], P('row')
- col_potential: float32 [128, 256], P('col')
Inputs may be any that keep to these rules, and one draw needn't show every extreme that they name: `block_lists`: the 16 column blocks of a row block are distinct. Among the row blocks of one index of row, at most 64 list entries name column blocks of one index of col, and exactly 64 for some index of col. Every column block is named by some row block of every index of row.
All inputs are finite; a program needn't handle non-finite values.
Results may differ from a plain program's by a relative error of at most 0.0003.
Values sent between devices are 32-bit elements; how exact they have to be, the bound alone decides.
No kernel may reach another device: no remote copies, remote signals or barrier semaphores. Data moves between devices by JAX's collectives and lax.ppermute only.
A program may use at most 64 MiB of HBM per device.

v0:
```python
import math

import jax
import jax.numpy as jnp
from jax import lax
from jax.sharding import PartitionSpec as P

DIM = 64
ITERS = 4
CAPACITY = 64


eps_reg = 0.05
neg_big = -1e30
group_slots = 8


def tile_partials(
    row_points, col_points, row_norms, col_norms, row_index, col_index, biases, over_columns
):
    row_tiles = row_points[row_index]
    col_tiles = col_points[col_index]
    inner_prod = jnp.einsum(
        "sdp,sdq->spq", row_tiles, col_tiles, preferred_element_type=jnp.float32
    )
    cost_tile = (
        row_norms[row_index][:, :, None] + col_norms[col_index][:, None, :] - 2.0 * inner_prod
    ) / DIM
    if over_columns:
        scores = (biases[:, None, :] - cost_tile) / eps_reg
        reduce_axis = 2
    else:
        scores = (biases[:, :, None] - cost_tile) / eps_reg
        reduce_axis = 1
    peak_vals = jnp.max(scores, axis=reduce_axis)
    totals = jnp.sum(jnp.exp(scores - jnp.expand_dims(peak_vals, reduce_axis)), axis=reduce_axis)
    return (peak_vals, totals)


def slot_partials(
    row_points, col_points, row_norms, col_norms, row_slot, col_slot, biases, over_columns
):
    groups = row_slot.shape[0] // group_slots
    block_size = row_points.shape[2]

    def one_group(members):
        return tile_partials(
            row_points,
            col_points,
            row_norms,
            col_norms,
            members[0],
            members[1],
            members[2],
            over_columns,
        )

    peak_parts, sum_parts = lax.map(
        one_group,
        (
            row_slot.reshape(groups, group_slots),
            col_slot.reshape(groups, group_slots),
            biases.reshape(groups, group_slots, block_size),
        ),
    )
    return (peak_parts.reshape(-1, block_size), sum_parts.reshape(-1, block_size))


def block_combine(peak_parts, sum_parts, members, slot_block, usable):
    block_peak = jnp.max(jnp.where(members[:, :, None], peak_parts[None, :, :], neg_big), axis=1)
    scale = jnp.where(usable[:, None], jnp.exp(peak_parts - block_peak[slot_block]), 0.0)
    block_sum = jnp.dot(
        members.astype(jnp.float32), sum_parts * scale, precision=lax.Precision.HIGHEST
    )
    return (block_peak, block_sum)


def potential_from(peak_vals, totals, log_mass):
    return eps_reg * (log_mass - (peak_vals + jnp.log(totals)))


def body(row_points, col_points, block_lists):
    row_blocks_here = row_points.shape[0]
    col_blocks_here = col_points.shape[0]
    block_size = row_points.shape[2]
    row_mass = -math.log(lax.axis_size("row") * row_blocks_here * block_size)
    col_mass = -math.log(lax.axis_size("col") * col_blocks_here * block_size)
    row_norms = jnp.sum(jnp.square(row_points.astype(jnp.float32)), axis=1)
    col_norms = jnp.sum(jnp.square(col_points.astype(jnp.float32)), axis=1)
    owned = (block_lists // col_blocks_here == lax.axis_index("col")).reshape(-1)
    entry_rank = jnp.cumsum(owned.astype(jnp.int32)) - 1
    slot_list = jnp.arange(CAPACITY, dtype=jnp.int32)
    picked = owned[None, :] & (entry_rank[None, :] == slot_list[:, None])
    entries = jnp.arange(owned.shape[0], dtype=jnp.int32)
    entry_of_slot = jnp.sum(jnp.where(picked, entries[None, :], 0), axis=1)
    usable = jnp.any(picked, axis=1)
    row_slot = entry_of_slot // block_lists.shape[1]
    col_slot = block_lists.reshape(-1)[entry_of_slot] % col_blocks_here
    row_members = (row_slot[None, :] == jnp.arange(row_blocks_here)[:, None]) & usable[None, :]
    col_members = (col_slot[None, :] == jnp.arange(col_blocks_here)[:, None]) & usable[None, :]
    col_potential = jnp.zeros((col_blocks_here, block_size), jnp.float32)
    row_potential = jnp.zeros((row_blocks_here, block_size), jnp.float32)
    for sweep in range(ITERS):
        peak_parts, sum_parts = slot_partials(
            row_points,
            col_points,
            row_norms,
            col_norms,
            row_slot,
            col_slot,
            col_potential[col_slot],
            True,
        )
        block_peak, block_sum = block_combine(peak_parts, sum_parts, row_members, row_slot, usable)
        whole_peak = lax.pmax(block_peak, "col")
        whole_sum = lax.psum(block_sum * jnp.exp(block_peak - whole_peak), "col")
        row_potential = potential_from(whole_peak, whole_sum, row_mass)
        peak_parts, sum_parts = slot_partials(
            row_points,
            col_points,
            row_norms,
            col_norms,
            row_slot,
            col_slot,
            row_potential[row_slot],
            False,
        )
        block_peak, block_sum = block_combine(peak_parts, sum_parts, col_members, col_slot, usable)
        whole_peak = lax.pmax(block_peak, "row")
        whole_sum = lax.psum(block_sum * jnp.exp(block_peak - whole_peak), "row")
        col_potential = potential_from(whole_peak, whole_sum, col_mass)
    return (row_potential, col_potential)


def solution(mesh):
    placed = (P("row", None, None), P("col", None, None), P("row", None))
    return jax.shard_map(
        body,
        mesh=mesh,
        in_specs=placed,
        out_specs=(P("row", None), P("col", None)),
        check_vma=False,
    )
```

profile of v0, /device:TPU:1, one launch (start us, length us, event | category | flops | bytes accessed | tf_op | source)
XLA Modules:
  0.0 1535.6 jit_solution(2969120463154943220)
XLA Ops:
  11.2 2.3 multiply_reduce_fusion
  14.2 32.7 %while.96 = (s32[]{:T(128)}, f32[8,8,256]{2,1,0:T(8,128)S(1)}, f32[8,8,256]{2,1,0:T(8,128)S(1)}, f32[8,8,256]{2,1,0:T(8,128)S(1)}, s32[8,8]{1,0:T(8,128)S(1)}, /...) while((s32[]{:T(128)}, f32[8,8,256]{2,1,0:T(8,128)S(1)}, ...), condition=%wide.region_9.10_spmd, body=%wide.region_6.9_spmd.sunk | while | flops 71825456 | bytes 5906877 | solution.py:58
  46.9 1.8 select_reduce_fusion.3
  48.8 1.5 gather_fusion.34
  50.3 139.6 %all-reduce.9.cloned.1.call-done = f32[64,256]{1,0:T(8,128)} async-done(((f32[64,256]{1,0:T(8,128)}), f32[64,256]{1,0:T(8,128)}) %all-reduce.9.cloned.1.call-update) | async-done | bytes 65552 | tf_op jit(solution)/shard_map/pmax | solution.py:115
  189.9 1.7 convolution_multiply_fusion.3
  191.7 141.8 %all-reduce.11.cloned.1.call-done = f32[64,256]{1,0:T(8,128)} async-done(((f32[64,256]{1,0:T(8,128)}), f32[64,256]{1,0:T(8,128)}) %all-reduce.11.cloned.1.call-update) | async-done | bytes 65552 | tf_op jit(solution)/shard_map/psum | solution.py:116
  335.1 32.8 %while.97 = (s32[]{:T(128)}, f32[8,8,256]{2,1,0:T(8,128)S(1)}, f32[8,8,256]{2,1,0:T(8,128)S(1)}, f32[8,8,256]{2,1,0:T(8,128)S(1)}, s32[8,8]{1,0:T(8,128)S(1)}, /...) while((s32[]{:T(128)}, f32[8,8,256]{2,1,0:T(8,128)S(1)}, ...), condition=%wide.region_16.17_spmd, body=%wide.region_13.16_spmd.sunk | while | flops 71825456 | bytes 5906877 | solution.py:58
  337.5 1.4 fusion.186
  341.6 1.4 fusion.186
  345.7 1.4 fusion.186
  358.0 1.4 fusion.186
  368.8 16.7 %pmax.57 = f32[4,256]{1,0:T(4,128)S(1)} all-reduce(f32[4,256]{1,0:T(4,128)S(1)} %select_reduce_fusion.7), channel_id=1, replica_groups=mesh['row'=8,'col'=32] {'row'}, use_global_device_ids=true, to_apply=%region_18.19 | all-reduce | flops 1024 | bytes 8192 | tf_op jit(solution)/shard_map/pmax | solution.py:129
  385.7 12.4 psum.57
  398.8 32.8 %while.98 = (s32[]{:T(128)}, f32[8,8,256]{2,1,0:T(8,128)S(1)}, f32[8,8,256]{2,1,0:T(8,128)S(1)}, f32[8,8,256]{2,1,0:T(8,128)S(1)}, s32[8,8]{1,0:T(8,128)S(1)}, /...) while((s32[]{:T(128)}, f32[8,8,256]{2,1,0:T(8,128)S(1)}, ...), condition=%wide.region_23.24_spmd, body=%wide.region_20.23_spmd.sunk | while | flops 71825456 | bytes 5906877 | solution.py:58
  431.6 1.8 select_reduce_fusion.2
  433.5 1.5 gather_fusion.38
  435.0 131.6 %all-reduce.13.cloned.1.call-done = f32[64,256]{1,0:T(8,128)} async-done(((f32[64,256]{1,0:T(8,128)}), f32[64,256]{1,0:T(8,128)}) %all-reduce.13.cloned.1.call-update) | async-done | bytes 65552 | tf_op jit(solution)/shard_map/pmax | solution.py:115
  566.6 1.7 convolution_multiply_fusion.2
  568.5 141.7 %all-reduce.15.cloned.1.call-done = f32[64,256]{1,0:T(8,128)} async-done(((f32[64,256]{1,0:T(8,128)}), f32[64,256]{1,0:T(8,128)}) %all-reduce.15.cloned.1.call-update) | async-done | bytes 65552 | tf_op jit(solution)/shard_map/psum | solution.py:116
  711.7 32.8 %while.99 = (s32[]{:T(128)}, f32[8,8,256]{2,1,0:T(8,128)S(1)}, f32[8,8,256]{2,1,0:T(8,128)S(1)}, f32[8,8,256]{2,1,0:T(8,128)S(1)}, s32[8,8]{1,0:T(8,128)S(1)}, /...) while((s32[]{:T(128)}, f32[8,8,256]{2,1,0:T(8,128)S(1)}, ...), condition=%wide.region_30.31_spmd, body=%wide.region_27.30_spmd.sunk | while | flops 71825456 | bytes 5906877 | solution.py:58
  714.1 1.4 fusion.196
  726.4 1.4 fusion.196
  738.7 1.4 fusion.196
  745.4 16.7 %pmax.59 = f32[4,256]{1,0:T(4,128)S(1)} all-reduce(f32[4,256]{1,0:T(4,128)S(1)} %select_reduce_fusion.6), channel_id=1, replica_groups=mesh['row'=8,'col'=32] {'row'}, use_global_device_ids=true, to_apply=%region_32.33 | all-reduce | flops 1024 | bytes 8192 | tf_op jit(solution)/shard_map/pmax | solution.py:129
  762.3 12.4 psum.59
  775.4 32.8 %while.100 = (s32[]{:T(128)}, f32[8,8,256]{2,1,0:T(8,128)S(1)}, f32[8,8,256]{2,1,0:T(8,128)S(1)}, f32[8,8,256]{2,1,0:T(8,128)S(1)}, s32[8,8]{1,0:T(8,128)S(1)}, ...) while((s32[]{:T(128)}, f32[8,8,256]{2,1,0:T(8,128)S(1)}, ...), condition=%wide.region_37.38_spmd, body=%wide.region_34.37_spmd.sunk | while | flops 71825456 | bytes 5906877 | solution.py:58
  808.2 1.8 select_reduce_fusion.1
  810.1 1.5 gather_fusion.42
  811.6 131.6 %all-reduce.17.cloned.1.call-done = f32[64,256]{1,0:T(8,128)} async-done(((f32[64,256]{1,0:T(8,128)}), f32[64,256]{1,0:T(8,128)}) %all-reduce.17.cloned.1.call-update) | async-done | bytes 65552 | tf_op jit(solution)/shard_map/pmax | solution.py:115
  943.2 1.7 convolution_multiply_fusion.1
  945.1 141.7 %all-reduce.19.cloned.1.call-done = f32[64,256]{1,0:T(8,128)} async-done(((f32[64,256]{1,0:T(8,128)}), f32[64,256]{1,0:T(8,128)}) %all-reduce.19.cloned.1.call-update) | async-done | bytes 65552 | tf_op jit(solution)/shard_map/psum | solution.py:116
  1088.3 32.8 %while.101 = (s32[]{:T(128)}, f32[8,8,256]{2,1,0:T(8,128)S(1)}, f32[8,8,256]{2,1,0:T(8,128)S(1)}, f32[8,8,256]{2,1,0:T(8,128)S(1)}, s32[8,8]{1,0:T(8,128)S(1)}, ...) while((s32[]{:T(128)}, f32[8,8,256]{2,1,0:T(8,128)S(1)}, ...), condition=%wide.region_44.45_spmd, body=%wide.region_41.44_spmd.sunk | while | flops 71825456 | bytes 5906877 | solution.py:58
  1090.7 1.4 fusion.206
  1094.8 1.4 fusion.206
  1107.1 1.4 fusion.206
  1119.4 1.4 fusion.206
  1122.0 16.7 %pmax.61 = f32[4,256]{1,0:T(4,128)S(1)} all-reduce(f32[4,256]{1,0:T(4,128)S(1)} %select_reduce_fusion.5), channel_id=1, replica_groups=mesh['row'=8,'col'=32] {'row'}, use_global_device_ids=true, to_apply=%region_46.47 | all-reduce | flops 1024 | bytes 8192 | tf_op jit(solution)/shard_map/pmax | solution.py:129
  1138.9 12.6 psum.61
  1152.2 32.8 %while.102 = (s32[]{:T(128)}, f32[8,8,256]{2,1,0:T(8,128)S(1)}, f32[8,8,256]{2,1,0:T(8,128)S(1)}, f32[8,8,256]{2,1,0:T(8,128)S(1)}, s32[8,8]{1,0:T(8,128)S(1)}, ...) while((s32[]{:T(128)}, f32[8,8,256]{2,1,0:T(8,128)S(1)}, ...), condition=%wide.region_51.52_spmd, body=%wide.region_48.51_spmd.sunk | while | flops 71825456 | bytes 5906877 | solution.py:58
  1185.0 1.8 select_reduce_fusion
  1186.9 1.5 gather_fusion.46
  1188.4 131.6 %all-reduce.21.cloned.1.call-done = f32[64,256]{1,0:T(8,128)} async-done(((f32[64,256]{1,0:T(8,128)}), f32[64,256]{1,0:T(8,128)}) %all-reduce.21.cloned.1.call-update) | async-done | bytes 65552 | tf_op jit(solution)/shard_map/pmax | solution.py:115
  1320.0 1.7 convolution_multiply_fusion
  1321.8 141.9 %all-reduce.23.cloned.1.call-done = f32[64,256]{1,0:T(8,128)} async-done(((f32[64,256]{1,0:T(8,128)}), f32[64,256]{1,0:T(8,128)}) %all-reduce.23.cloned.1.call-update) | async-done | bytes 65552 | tf_op jit(solution)/shard_map/psum | solution.py:116
  1465.3 32.7 %while.103 = (s32[]{:T(128)}, f32[8,8,256]{2,1,0:T(8,128)S(1)}, f32[8,8,256]{2,1,0:T(8,128)S(1)}, f32[8,8,256]{2,1,0:T(8,128)S(1)}, s32[8,8]{1,0:T(8,128)S(1)}, ...) while((s32[]{:T(128)}, f32[8,8,256]{2,1,0:T(8,128)S(1)}, ...), condition=%wide.region_58.59_spmd, body=%wide.region_55.58_spmd.sunk | while | flops 71825456 | bytes 5906877 | solution.py:58
  1498.7 16.8 %pmax.63 = f32[4,256]{1,0:T(4,128)S(1)} all-reduce(f32[4,256]{1,0:T(4,128)S(1)} %select_reduce_fusion.4), channel_id=1, replica_groups=mesh['row'=8,'col'=32] {'row'}, use_global_device_ids=true, to_apply=%region_60.61 | all-reduce | flops 1024 | bytes 8192 | tf_op jit(solution)/shard_map/pmax | solution.py:129
  1515.7 12.4 psum.63
  (852 shorter events, 258.8 us)
Async XLA Ops:
  7.2 7.0 copy-start.1
  7.2 6.3 copy-start
  7.2 182.7 %all-reduce.9.cloned.1.call-start = ((), (), s32[]{:S(2)}) async-start(), calls=%async_computation | async-start | bytes 131072 | tf_op jit(solution)/shard_map/pmax | solution.py:115
  48.8 284.8 %all-reduce.11.cloned.1.call-start = ((), (), s32[]{:S(2)}) async-start(), calls=%async_computation.1 | async-start | bytes 131072 | tf_op jit(solution)/shard_map/psum | solution.py:116
  191.7 375.0 %all-reduce.13.cloned.1.call-start = ((), (), s32[]{:S(2)}) async-start(), calls=%async_computation.2 | async-start | bytes 131072 | tf_op jit(solution)/shard_map/pmax | solution.py:115
  433.5 276.7 %all-reduce.15.cloned.1.call-start = ((), (), s32[]{:S(2)}) async-start(), calls=%async_computation.3 | async-start | bytes 131072 | tf_op jit(solution)/shard_map/psum | solution.py:116
  568.4 374.8 %all-reduce.17.cloned.1.call-start = ((), (), s32[]{:S(2)}) async-start(), calls=%async_computation.4 | async-start | bytes 131072 | tf_op jit(solution)/shard_map/pmax | solution.py:115
  810.1 276.7 %all-reduce.19.cloned.1.call-start = ((), (), s32[]{:S(2)}) async-start(), calls=%async_computation.5 | async-start | bytes 131072 | tf_op jit(solution)/shard_map/psum | solution.py:116
  945.0 375.0 %all-reduce.21.cloned.1.call-start = ((), (), s32[]{:S(2)}) async-start(), calls=%async_computation.6 | async-start | bytes 131072 | tf_op jit(solution)/shard_map/pmax | solution.py:115
  1186.8 276.8 %all-reduce.23.cloned.1.call-start = ((), (), s32[]{:S(2)}) async-start(), calls=%async_computation.7 | async-start | bytes 131072 | tf_op jit(solution)/shard_map/psum | solution.py:116
  1464.6 0.7 copy-start.2
Sparse Core Ops, SparseCore 0:
  48.9 140.9 all-reduce.8
  193.9 139.5 all-reduce.10
  433.6 132.9 all-reduce.12
  570.5 139.5 all-reduce.14
  810.2 132.9 all-reduce.16
  947.1 139.5 all-reduce.18
  1187.0 133.0 all-reduce.20
  1324.0 139.5 all-reduce.22
where the time goes:
time: 1540 us
  waiting for transfers between devices  1100 us (71%)
  local copies, waits for them, and re-layouts  162 us (11%)
  blocking collectives  117 us (8%)
  matrix products  97.4 us (6%)
  other arithmetic  37 us (2%)
    psum x4, waiting for transfers between devices, body(): whole_sum = lax.psum(block_sum * jnp.exp(block_peak - whole_peak), 'col')  567 us
    pmax x4, waiting for transfers between devices, body(): whole_peak = lax.pmax(block_peak, 'col')  534 us
    dot_general x64, matrix products, tile_partials(): jnp.einsum('sdp,sdq->spq', row_tiles, col_tiles, preferred_element_type=j...  89.7 us
    pmax x4, blocking collectives, body(): whole_peak = lax.pmax(block_peak, 'row')  67 us
    psum x4, blocking collectives, body(): whole_sum = lax.psum(block_sum * jnp.exp(block_peak - whole_peak), 'row')  49.8 us
    gather x64, local copies, waits for them, and re-layouts, tile_partials(): col_tiles = col_points[col_index]  36.1 us
    gather x64, local copies, waits for them, and re-layouts, tile_partials(): row_tiles = row_points[row_index]  36.1 us
    gather x64, local copies, waits for them, and re-layouts, tile_partials(): row_norms[row_index][:, :, None] + col_norms[col_index][:, None, :]  36 us
  transfers between devices with their start and end apart: 8, of which 8 were waited for; matrix products, arithmetic and copies ran while one was open for 0% of the time, Pallas kernels for 0%

commit v1 on v0

--- a/solution.py
+++ b/solution.py
@@ -75,6 +75,27 @@
     return (block_peak, block_sum)
 
 
+def lse_allreduce(peak_vals, totals, axis):
+    size = lax.axis_size(axis)
+    if size & (size - 1):
+        whole_peak = lax.pmax(peak_vals, axis)
+        whole_sum = lax.psum(totals * jnp.exp(peak_vals - whole_peak), axis)
+        return (whole_peak, whole_sum)
+    here = lax.axis_index(axis)
+    pair = jnp.stack([peak_vals, totals])
+    step = 1
+    while step < size:
+        other = lax.ppermute(pair, axis, [(i, i ^ step) for i in range(size)])
+        low_side = (here // step) % 2 == 0
+        lo = jnp.where(low_side, pair, other)
+        hi = jnp.where(low_side, other, pair)
+        top = jnp.maximum(lo[0], hi[0])
+        total = lo[1] * jnp.exp(lo[0] - top) + hi[1] * jnp.exp(hi[0] - top)
+        pair = jnp.stack([top, total])
+        step *= 2
+    return (pair[0], pair[1])
+
+
 def potential_from(peak_vals, totals, log_mass):
     return eps_reg * (log_mass - (peak_vals + jnp.log(totals)))
 
@@ -112,8 +133,7 @@
             True,
         )
         block_peak, block_sum = block_combine(peak_parts, sum_parts, row_members, row_slot, usable)
-        whole_peak = lax.pmax(block_peak, "col")
-        whole_sum = lax.psum(block_sum * jnp.exp(block_peak - whole_peak), "col")
+        whole_peak, whole_sum = lse_allreduce(block_peak, block_sum, "col")
         row_potential = potential_from(whole_peak, whole_sum, row_mass)
         peak_parts, sum_parts = slot_partials(
             row_points,
@@ -126,8 +146,7 @@
             False,
         )
         block_peak, block_sum = block_combine(peak_parts, sum_parts, col_members, col_slot, usable)
-        whole_peak = lax.pmax(block_peak, "row")
-        whole_sum = lax.psum(block_sum * jnp.exp(block_peak - whole_peak), "row")
+        whole_peak, whole_sum = lse_allreduce(block_peak, block_sum, "row")
         col_potential = potential_from(whole_peak, whole_sum, col_mass)
     return (row_potential, col_potential)
 

time: 1540 us -> 480 us (0.31)
  waiting for transfers between devices: 1100 us -> 88.6 us
  blocking collectives: 117 us -> 0 us
  starting transfers between devices: 0.33 us -> 99.3 us
    psum x4 -> x0, waiting for transfers between devices: 567 us -> none  [body(): whole_sum = lax.psum(block_sum * jnp.exp(block_peak - whole_peak), 'col')]
    pmax x4 -> x0, waiting for transfers between devices: 534 us -> none  [body(): whole_peak = lax.pmax(block_peak, 'col')]
    ppermute x0 -> x32, starting transfers between devices: none -> 99.3 us  [lse_allreduce(): other = lax.ppermute(pair, axis, [(i, i ^ step) for i in range(size)])]
    ppermute x0 -> x32, waiting for transfers between devices: none -> 88.6 us  [lse_allreduce(): other = lax.ppermute(pair, axis, [(i, i ^ step) for i in range(size)])]
    pmax x4 -> x0, blocking collectives: 67 us -> none  [body(): whole_peak = lax.pmax(block_peak, 'row')]
    psum x4 -> x0, blocking collectives: 49.8 us -> none  [body(): whole_sum = lax.psum(block_sum * jnp.exp(block_peak - whole_peak), 'row')]
  transfers between devices with their start and end apart: 8 -> 32, of which waited for: 8 -> 32; matrix products, arithmetic and copies ran while one was open for 0% -> 0% of each run, Pallas kernels for 0% -> 0%
where the time goes in v1:
time: 480 us; the launch traced here: 478 us
  local copies, waits for them, and re-layouts  158 us (33%)
  starting transfers between devices  99.3 us (21%)
  matrix products  91.2 us (19%)
  waiting for transfers between devices  88.6 us (18%)
  other arithmetic  32.2 us (7%)
  loops' own time  6.12 us (1%)
    ppermute x32, starting transfers between devices, lse_allreduce(): other = lax.ppermute(pair, axis, [(i, i ^ step) for i in range(size)])  99.3 us
    dot_general x64, matrix products, tile_partials(): jnp.einsum('sdp,sdq->spq', row_tiles, col_tiles, preferred_element_type=j...  89.4 us
    ppermute x32, waiting for transfers between devices, lse_allreduce(): other = lax.ppermute(pair, axis, [(i, i ^ step) for i in range(size)])  88.6 us
    gather x64, local copies, waits for them, and re-layouts, tile_partials(): row_tiles = row_points[row_index]  36.1 us
    gather x64, local copies, waits for them, and re-layouts, tile_partials(): col_tiles = col_points[col_index]  36.1 us
    gather x64, local copies, waits for them, and re-layouts, tile_partials(): col_norms[col_index][:, None, :]  36 us
    gather x64, local copies, waits for them, and re-layouts, tile_partials(): row_norms[row_index][:, :, None] + col_norms[col_index][:, None, :]  36 us
    reduce_sum x64, other arithmetic, tile_partials(): jnp.sum(jnp.exp(scores - jnp.expand_dims(peak_vals, reduce_axis)), axis=r...  18.8 us
  transfers between devices with their start and end apart: 32, of which 32 were waited for; matrix products, arithmetic and copies ran while one was open for 0% of the time, Pallas kernels for 0%

profile of v1, /device:TPU:1, one launch (start us, length us, event | category | flops | bytes accessed | tf_op | source)
XLA Modules:
  0.0 477.5 jit_solution(5514443871032759418)
XLA Ops:
  4.6 2.3 multiply_reduce_fusion
  7.7 32.7 %while.96 = (s32[]{:T(128)}, f32[8,8,256]{2,1,0:T(8,128)S(1)}, f32[8,8,256]{2,1,0:T(8,128)S(1)}, f32[8,8,256]{2,1,0:T(8,128)S(1)}, s32[8,8]{1,0:T(8,128)S(1)}, /...) while((s32[]{:T(128)}, f32[8,8,256]{2,1,0:T(8,128)S(1)}, ...), condition=%wide.region_9.10_spmd, body=%wide.region_6.9_spmd.sunk | while | flops 71825456 | bytes 5906877 | solution.py:58
  42.5 2.2 collective-permute-start
  44.7 2.4 collective-permute-done
  47.1 3.7 collective-permute-start.1
  50.9 2.4 collective-permute-done.1
  55.1 2.4 collective-permute-done.2
  57.5 3.1 collective-permute-start.3
  60.6 2.7 collective-permute-done.3
  63.4 7.3 %collective-permute-start.4 = (f32[2,64,256]{2,1,0:T(8,128)S(1)}, f32[2,64,256]{2,1,0:T(8,128)S(1)}, u32[]{:S(2)}, u32[]{:S(2)}) collective-permute-start(f32[2,64,256]{2,1,0:T(8,128)S(1)} %pad_maximum_fusion.4), channel_id=1, source_target_pairs={{0,16},{1,17},{2,18},{3,19},{4,20},{5,21},{6,22},{7,23},{8,24},{9,... | collective-permute-start | bytes 393224 | tf_op jit(solution)/shard_map/ppermute | solution.py:88
  70.7 3.2 collective-permute-done.4
  74.6 32.7 %while.97 = (s32[]{:T(128)}, f32[8,8,256]{2,1,0:T(8,128)S(1)}, f32[8,8,256]{2,1,0:T(8,128)S(1)}, f32[8,8,256]{2,1,0:T(8,128)S(1)}, s32[8,8]{1,0:T(8,128)S(1)}, /...) while((s32[]{:T(128)}, f32[8,8,256]{2,1,0:T(8,128)S(1)}, ...), condition=%wide.region_14.15_spmd, body=%wide.region_11.14_spmd.sunk | while | flops 71825456 | bytes 5906877 | solution.py:58
  108.3 6.5 %collective-permute-start.5 = (f32[2,4,256]{2,1,0:T(4,128)S(1)}, f32[2,4,256]{2,1,0:T(4,128)S(1)}, u32[]{:S(2)}, u32[]{:S(2)}) collective-permute-start(f32[2,4,256]{2,1,0:T(4,128)S(1)} %pad_maximum_fusion.20), channel_id=1, source_target_pairs={{0,32},{32,0},{64,96},{96,64},{128,160},{160,128},{192,224},{224,1... | collective-permute-start | bytes 24584 | tf_op jit(solution)/shard_map/ppermute | solution.py:88
  118.3 2.8 collective-permute-start.7
  123.1 32.8 %while.98 = (s32[]{:T(128)}, f32[8,8,256]{2,1,0:T(8,128)S(1)}, f32[8,8,256]{2,1,0:T(8,128)S(1)}, f32[8,8,256]{2,1,0:T(8,128)S(1)}, s32[8,8]{1,0:T(8,128)S(1)}, /...) while((s32[]{:T(128)}, f32[8,8,256]{2,1,0:T(8,128)S(1)}, ...), condition=%wide.region_19.20_spmd, body=%wide.region_16.19_spmd.sunk | while | flops 71825456 | bytes 5906877 | solution.py:58
  159.4 2.5 collective-permute-done.8
  162.0 3.2 collective-permute-start.9
  165.2 3.7 collective-permute-done.9
  169.1 3.8 collective-permute-done.10
  173.5 5.5 %collective-permute-done.11 = f32[2,64,256]{2,1,0:T(8,128)S(1)} collective-permute-done((f32[2,64,256]{2,1,0:T(8,128)S(1)}, f32[2,64,256]{2,1,0:T(8,128)S(1)}, u32[]{:S(2)}, u32[]{:S(2)}) %collective-permute-start.11) | collective-permute-done | bytes 131104 | tf_op jit(solution)/shard_map/ppermute | solution.py:88
  179.1 5.7 %collective-permute-start.12 = (f32[2,64,256]{2,1,0:T(8,128)S(1)}, f32[2,64,256]{2,1,0:T(8,128)S(1)}, u32[]{:S(2)}, u32[]{:S(2)}) collective-permute-start(f32[2,64,256]{2,1,0:T(8,128)S(1)} %pad_maximum_fusion.9), channel_id=1, source_target_pairs={{0,16},{1,17},{2,18},{3,19},{4,20},{5,21},{6,22},{7,23},{8,24},{9,... | collective-permute-start | bytes 393224 | tf_op jit(solution)/shard_map/ppermute | solution.py:88
  184.9 3.8 collective-permute-done.12
  189.4 32.7 %while.99 = (s32[]{:T(128)}, f32[8,8,256]{2,1,0:T(8,128)S(1)}, f32[8,8,256]{2,1,0:T(8,128)S(1)}, f32[8,8,256]{2,1,0:T(8,128)S(1)}, s32[8,8]{1,0:T(8,128)S(1)}, /...) while((s32[]{:T(128)}, f32[8,8,256]{2,1,0:T(8,128)S(1)}, ...), condition=%wide.region_24.25_spmd, body=%wide.region_21.24_spmd.sunk | while | flops 71825456 | bytes 5906877 | solution.py:58
  223.1 8.6 %collective-permute-start.13 = (f32[2,4,256]{2,1,0:T(4,128)S(1)}, f32[2,4,256]{2,1,0:T(4,128)S(1)}, u32[]{:S(2)}, u32[]{:S(2)}) collective-permute-start(f32[2,4,256]{2,1,0:T(4,128)S(1)} %pad_maximum_fusion.23), channel_id=1, source_target_pairs={{0,32},{32,0},{64,96},{96,64},{128,160},{160,128},{192,224},{224,1... | collective-permute-start | bytes 24584 | tf_op jit(solution)/shard_map/ppermute | solution.py:88
  235.2 2.8 collective-permute-start.15
  240.0 32.7 %while.100 = (s32[]{:T(128)}, f32[8,8,256]{2,1,0:T(8,128)S(1)}, f32[8,8,256]{2,1,0:T(8,128)S(1)}, f32[8,8,256]{2,1,0:T(8,128)S(1)}, s32[8,8]{1,0:T(8,128)S(1)}, ...) while((s32[]{:T(128)}, f32[8,8,256]{2,1,0:T(8,128)S(1)}, ...), condition=%wide.region_29.30_spmd, body=%wide.region_26.29_spmd.sunk | while | flops 71825456 | bytes 5906877 | solution.py:58
  274.8 3.1 collective-permute-start.16
  277.9 2.4 collective-permute-done.16
  280.4 3.2 collective-permute-start.17
  283.6 3.2 collective-permute-done.17
  287.0 3.8 collective-permute-done.18
  291.4 5.5 %collective-permute-done.19 = f32[2,64,256]{2,1,0:T(8,128)S(1)} collective-permute-done((f32[2,64,256]{2,1,0:T(8,128)S(1)}, f32[2,64,256]{2,1,0:T(8,128)S(1)}, u32[]{:S(2)}, u32[]{:S(2)}) %collective-permute-start.19) | collective-permute-done | bytes 131104 | tf_op jit(solution)/shard_map/ppermute | solution.py:88
  297.0 4.4 collective-permute-start.20
  301.4 4.0 collective-permute-done.20
  306.2 32.7 %while.101 = (s32[]{:T(128)}, f32[8,8,256]{2,1,0:T(8,128)S(1)}, f32[8,8,256]{2,1,0:T(8,128)S(1)}, f32[8,8,256]{2,1,0:T(8,128)S(1)}, s32[8,8]{1,0:T(8,128)S(1)}, ...) while((s32[]{:T(128)}, f32[8,8,256]{2,1,0:T(8,128)S(1)}, ...), condition=%wide.region_34.35_spmd, body=%wide.region_31.34_spmd.sunk | while | flops 71825456 | bytes 5906877 | solution.py:58
  339.8 11.6 %collective-permute-start.21 = (f32[2,4,256]{2,1,0:T(4,128)S(1)}, f32[2,4,256]{2,1,0:T(4,128)S(1)}, u32[]{:S(2)}, u32[]{:S(2)}) collective-permute-start(f32[2,4,256]{2,1,0:T(4,128)S(1)} %pad_maximum_fusion.26), channel_id=1, source_target_pairs={{0,32},{32,0},{64,96},{96,64},{128,160},{160,128},{192,224},{224,1... | collective-permute-start | bytes 24584 | tf_op jit(solution)/shard_map/ppermute | solution.py:88
  355.2 4.0 collective-permute-done.23
  359.9 32.8 %while.102 = (s32[]{:T(128)}, f32[8,8,256]{2,1,0:T(8,128)S(1)}, f32[8,8,256]{2,1,0:T(8,128)S(1)}, f32[8,8,256]{2,1,0:T(8,128)S(1)}, s32[8,8]{1,0:T(8,128)S(1)}, ...) while((s32[]{:T(128)}, f32[8,8,256]{2,1,0:T(8,128)S(1)}, ...), condition=%wide.region_39.40_spmd, body=%wide.region_36.39_spmd.sunk | while | flops 71825456 | bytes 5906877 | solution.py:58
  396.4 2.4 collective-permute-done.24
  398.9 3.2 collective-permute-start.25
  402.1 3.4 collective-permute-done.25
  405.7 3.8 collective-permute-done.26
  409.8 5.8 %collective-permute-done.27 = f32[2,64,256]{2,1,0:T(8,128)S(1)} collective-permute-done((f32[2,64,256]{2,1,0:T(8,128)S(1)}, f32[2,64,256]{2,1,0:T(8,128)S(1)}, u32[]{:S(2)}, u32[]{:S(2)}) %collective-permute-start.27) | collective-permute-done | bytes 131104 | tf_op jit(solution)/shard_map/ppermute | solution.py:88
  415.7 2.8 collective-permute-start.28
  418.5 5.8 %collective-permute-done.28 = f32[2,64,256]{2,1,0:T(8,128)S(1)} collective-permute-done((f32[2,64,256]{2,1,0:T(8,128)S(1)}, f32[2,64,256]{2,1,0:T(8,128)S(1)}, u32[]{:S(2)}, u32[]{:S(2)}) %collective-permute-start.28) | collective-permute-done | bytes 131104 | tf_op jit(solution)/shard_map/ppermute | solution.py:88
  425.1 32.8 %while.103 = (s32[]{:T(128)}, f32[8,8,256]{2,1,0:T(8,128)S(1)}, f32[8,8,256]{2,1,0:T(8,128)S(1)}, f32[8,8,256]{2,1,0:T(8,128)S(1)}, s32[8,8]{1,0:T(8,128)S(1)}, ...) while((s32[]{:T(128)}, f32[8,8,256]{2,1,0:T(8,128)S(1)}, ...), condition=%wide.region_44.45_spmd, body=%wide.region_41.44_spmd.sunk | while | flops 71825456 | bytes 5906877 | solution.py:58
  458.9 10.4 %collective-permute-start.29 = (f32[2,4,256]{2,1,0:T(4,128)S(1)}, f32[2,4,256]{2,1,0:T(4,128)S(1)}, u32[]{:S(2)}, u32[]{:S(2)}) collective-permute-start(f32[2,4,256]{2,1,0:T(4,128)S(1)} %pad_maximum_fusion.29), channel_id=1, source_target_pairs={{0,32},{32,0},{64,96},{96,64},{128,160},{160,128},{192,224},{224,1... | collective-permute-start | bytes 24584 | tf_op jit(solution)/shard_map/ppermute | solution.py:88
  472.8 2.8 collective-permute-start.31
  (972 shorter events, 303.7 us)
Async XLA Ops:
  0.6 7.0 %copy-start.1 = (bf16[64,64,256]{2,1,0:T(8,128)(2,1)S(1)}, bf16[64,64,256]{2,1,0:T(8,128)(2,1)}, u32[]{:S(2)}) copy-start(bf16[64,64,256]{2,1,0:T(8,128)(2,1)} %param.19) | copy-start | bytes 6291460
  0.6 6.3 %copy-start = (bf16[4,64,256]{2,1,0:T(8,128)(2,1)S(1)}, bf16[4,64,256]{2,1,0:T(8,128)(2,1)}, u32[]{:S(2)}) copy-start(bf16[4,64,256]{2,1,0:T(8,128)(2,1)} %param.20) | copy-start | bytes 393220
  42.5 4.6 collective-permute-start
  47.1 6.1 %collective-permute-start.1 = (f32[2,64,256]{2,1,0:T(8,128)S(1)}, f32[2,64,256]{2,1,0:T(8,128)S(1)}, u32[]{:S(2)}, u32[]{:S(2)}) collective-permute-start(f32[2,64,256]{2,1,0:T(8,128)S(1)} %pad_maximum_fusion.1), channel_id=1, source_target_pairs={{0,2},{1,3},{2,0},{3,1},{4,6},{5,7},{6,4},{7,5},{8,10},{9,11},{10,... | collective-permute-start | bytes 393224 | tf_op jit(solution)/shard_map/ppermute | solution.py:88
  53.3 4.1 collective-permute-start.2
  57.5 5.7 %collective-permute-start.3 = (f32[2,64,256]{2,1,0:T(8,128)S(1)}, f32[2,64,256]{2,1,0:T(8,128)S(1)}, u32[]{:S(2)}, u32[]{:S(2)}) collective-permute-start(f32[2,64,256]{2,1,0:T(8,128)S(1)} %pad_maximum_fusion.3), channel_id=1, source_target_pairs={{0,8},{1,9},{2,10},{3,11},{4,12},{5,13},{6,14},{7,15},{8,0},{9,1},... | collective-permute-start | bytes 393224 | tf_op jit(solution)/shard_map/ppermute | solution.py:88
  63.4 10.5 %collective-permute-start.4 = (f32[2,64,256]{2,1,0:T(8,128)S(1)}, f32[2,64,256]{2,1,0:T(8,128)S(1)}, u32[]{:S(2)}, u32[]{:S(2)}) collective-permute-start(f32[2,64,256]{2,1,0:T(8,128)S(1)} %pad_maximum_fusion.4), channel_id=1, source_target_pairs={{0,16},{1,17},{2,18},{3,19},{4,20},{5,21},{6,22},{7,23},{8,24},{9,... | collective-permute-start | bytes 393224 | tf_op jit(solution)/shard_map/ppermute | solution.py:88
  108.3 7.3 %collective-permute-start.5 = (f32[2,4,256]{2,1,0:T(4,128)S(1)}, f32[2,4,256]{2,1,0:T(4,128)S(1)}, u32[]{:S(2)}, u32[]{:S(2)}) collective-permute-start(f32[2,4,256]{2,1,0:T(4,128)S(1)} %pad_maximum_fusion.20), channel_id=1, source_target_pairs={{0,32},{32,0},{64,96},{96,64},{128,160},{160,128},{192,224},{224,1... | collective-permute-start | bytes 24584 | tf_op jit(solution)/shard_map/ppermute | solution.py:88
  115.7 2.6 collective-permute-start.6
  118.3 4.1 collective-permute-start.7
  158.0 3.9 collective-permute-start.8
  162.0 6.9 %collective-permute-start.9 = (f32[2,64,256]{2,1,0:T(8,128)S(1)}, f32[2,64,256]{2,1,0:T(8,128)S(1)}, u32[]{:S(2)}, u32[]{:S(2)}) collective-permute-start(f32[2,64,256]{2,1,0:T(8,128)S(1)} %pad_maximum_fusion.6), channel_id=1, source_target_pairs={{0,2},{1,3},{2,0},{3,1},{4,6},{5,7},{6,4},{7,5},{8,10},{9,11},{10,... | collective-permute-start | bytes 393224 | tf_op jit(solution)/shard_map/ppermute | solution.py:88
  169.0 3.9 collective-permute-start.10
  173.0 6.1 %collective-permute-start.11 = (f32[2,64,256]{2,1,0:T(8,128)S(1)}, f32[2,64,256]{2,1,0:T(8,128)S(1)}, u32[]{:S(2)}, u32[]{:S(2)}) collective-permute-start(f32[2,64,256]{2,1,0:T(8,128)S(1)} %pad_maximum_fusion.8), channel_id=1, source_target_pairs={{0,8},{1,9},{2,10},{3,11},{4,12},{5,13},{6,14},{7,15},{8,0},{9,1},... | collective-permute-start | bytes 393224 | tf_op jit(solution)/shard_map/ppermute | solution.py:88
  179.1 9.5 %collective-permute-start.12 = (f32[2,64,256]{2,1,0:T(8,128)S(1)}, f32[2,64,256]{2,1,0:T(8,128)S(1)}, u32[]{:S(2)}, u32[]{:S(2)}) collective-permute-start(f32[2,64,256]{2,1,0:T(8,128)S(1)} %pad_maximum_fusion.9), channel_id=1, source_target_pairs={{0,16},{1,17},{2,18},{3,19},{4,20},{5,21},{6,22},{7,23},{8,24},{9,... | collective-permute-start | bytes 393224 | tf_op jit(solution)/shard_map/ppermute | solution.py:88
  223.1 9.4 %collective-permute-start.13 = (f32[2,4,256]{2,1,0:T(4,128)S(1)}, f32[2,4,256]{2,1,0:T(4,128)S(1)}, u32[]{:S(2)}, u32[]{:S(2)}) collective-permute-start(f32[2,4,256]{2,1,0:T(4,128)S(1)} %pad_maximum_fusion.23), channel_id=1, source_target_pairs={{0,32},{32,0},{64,96},{96,64},{128,160},{160,128},{192,224},{224,1... | collective-permute-start | bytes 24584 | tf_op jit(solution)/shard_map/ppermute | solution.py:88
  232.5 2.6 collective-permute-start.14
  235.2 4.1 collective-permute-start.15
  274.8 5.5 %collective-permute-start.16 = (f32[2,64,256]{2,1,0:T(8,128)S(1)}, f32[2,64,256]{2,1,0:T(8,128)S(1)}, u32[]{:S(2)}, u32[]{:S(2)}) collective-permute-start(f32[2,64,256]{2,1,0:T(8,128)S(1)} %pad_maximum_fusion.10), channel_id=1, source_target_pairs={{0,1},{1,0},{2,3},{3,2},{4,5},{5,4},{6,7},{7,6},{8,9},{9,8},{10,11... | collective-permute-start | bytes 393224 | tf_op jit(solution)/shard_map/ppermute | solution.py:88
  280.4 6.4 %collective-permute-start.17 = (f32[2,64,256]{2,1,0:T(8,128)S(1)}, f32[2,64,256]{2,1,0:T(8,128)S(1)}, u32[]{:S(2)}, u32[]{:S(2)}) collective-permute-start(f32[2,64,256]{2,1,0:T(8,128)S(1)} %pad_maximum_fusion.11), channel_id=1, source_target_pairs={{0,2},{1,3},{2,0},{3,1},{4,6},{5,7},{6,4},{7,5},{8,10},{9,11},{10,... | collective-permute-start | bytes 393224 | tf_op jit(solution)/shard_map/ppermute | solution.py:88
  286.9 3.9 collective-permute-start.18
  290.9 6.1 %collective-permute-start.19 = (f32[2,64,256]{2,1,0:T(8,128)S(1)}, f32[2,64,256]{2,1,0:T(8,128)S(1)}, u32[]{:S(2)}, u32[]{:S(2)}) collective-permute-start(f32[2,64,256]{2,1,0:T(8,128)S(1)} %pad_maximum_fusion.13), channel_id=1, source_target_pairs={{0,8},{1,9},{2,10},{3,11},{4,12},{5,13},{6,14},{7,15},{8,0},{9,1},... | collective-permute-start | bytes 393224 | tf_op jit(solution)/shard_map/ppermute | solution.py:88
  297.0 8.4 %collective-permute-start.20 = (f32[2,64,256]{2,1,0:T(8,128)S(1)}, f32[2,64,256]{2,1,0:T(8,128)S(1)}, u32[]{:S(2)}, u32[]{:S(2)}) collective-permute-start(f32[2,64,256]{2,1,0:T(8,128)S(1)} %pad_maximum_fusion.14), channel_id=1, source_target_pairs={{0,16},{1,17},{2,18},{3,19},{4,20},{5,21},{6,22},{7,23},{8,24},{9,... | collective-permute-start | bytes 393224 | tf_op jit(solution)/shard_map/ppermute | solution.py:88
  339.8 12.4 %collective-permute-start.21 = (f32[2,4,256]{2,1,0:T(4,128)S(1)}, f32[2,4,256]{2,1,0:T(4,128)S(1)}, u32[]{:S(2)}, u32[]{:S(2)}) collective-permute-start(f32[2,4,256]{2,1,0:T(4,128)S(1)} %pad_maximum_fusion.26), channel_id=1, source_target_pairs={{0,32},{32,0},{64,96},{96,64},{128,160},{160,128},{192,224},{224,1... | collective-permute-start | bytes 24584 | tf_op jit(solution)/shard_map/ppermute | solution.py:88
  352.3 2.8 collective-permute-start.22
  355.1 4.1 collective-permute-start.23
  394.9 3.9 collective-permute-start.24
  398.9 6.6 %collective-permute-start.25 = (f32[2,64,256]{2,1,0:T(8,128)S(1)}, f32[2,64,256]{2,1,0:T(8,128)S(1)}, u32[]{:S(2)}, u32[]{:S(2)}) collective-permute-start(f32[2,64,256]{2,1,0:T(8,128)S(1)} %pad_maximum_fusion.16), channel_id=1, source_target_pairs={{0,2},{1,3},{2,0},{3,1},{4,6},{5,7},{6,4},{7,5},{8,10},{9,11},{10,... | collective-permute-start | bytes 393224 | tf_op jit(solution)/shard_map/ppermute | solution.py:88
  405.6 3.9 collective-permute-start.26
  409.5 6.1 %collective-permute-start.27 = (f32[2,64,256]{2,1,0:T(8,128)S(1)}, f32[2,64,256]{2,1,0:T(8,128)S(1)}, u32[]{:S(2)}, u32[]{:S(2)}) collective-permute-start(f32[2,64,256]{2,1,0:T(8,128)S(1)} %pad_maximum_fusion.18), channel_id=1, source_target_pairs={{0,8},{1,9},{2,10},{3,11},{4,12},{5,13},{6,14},{7,15},{8,0},{9,1},... | collective-permute-start | bytes 393224 | tf_op jit(solution)/shard_map/ppermute | solution.py:88
  415.7 8.6 %collective-permute-start.28 = (f32[2,64,256]{2,1,0:T(8,128)S(1)}, f32[2,64,256]{2,1,0:T(8,128)S(1)}, u32[]{:S(2)}, u32[]{:S(2)}) collective-permute-start(f32[2,64,256]{2,1,0:T(8,128)S(1)} %pad_maximum_fusion.19), channel_id=1, source_target_pairs={{0,16},{1,17},{2,18},{3,19},{4,20},{5,21},{6,22},{7,23},{8,24},{9,... | collective-permute-start | bytes 393224 | tf_op jit(solution)/shard_map/ppermute | solution.py:88
  424.4 0.7 copy-start.2
  458.9 11.3 %collective-permute-start.29 = (f32[2,4,256]{2,1,0:T(4,128)S(1)}, f32[2,4,256]{2,1,0:T(4,128)S(1)}, u32[]{:S(2)}, u32[]{:S(2)}) collective-permute-start(f32[2,4,256]{2,1,0:T(4,128)S(1)} %pad_maximum_fusion.29), channel_id=1, source_target_pairs={{0,32},{32,0},{64,96},{96,64},{128,160},{160,128},{192,224},{224,1... | collective-permute-start | bytes 24584 | tf_op jit(solution)/shard_map/ppermute | solution.py:88
  470.2 2.6 collective-permute-start.30
  472.8 4.1 collective-permute-start.31

commit v2 on v1

v2 whole, which is shorter than its diff:
```python
import math

import jax
import jax.numpy as jnp
from jax import lax
from jax.experimental import pallas as pl
from jax.experimental.pallas import tpu as pltpu
from jax.sharding import PartitionSpec as P

DIM = 64
ITERS = 4
CAPACITY = 64
AUG = 128


eps_reg = 0.05
neg_big = -1e30
ip_scale = 2.0 / (DIM * eps_reg)


def slot_kernel(lhs_slot, rhs_slot, lhs_ref, rhs_ref, peak_ref, sum_ref):
    def one_slot(k, carry):
        tile = jnp.dot(
            lhs_ref[lhs_slot[k]], rhs_ref[rhs_slot[k]], preferred_element_type=jnp.float32
        )
        scores = tile * ip_scale
        peak = jnp.max(scores, axis=0, keepdims=True)
        peak_ref[k] = peak
        sum_ref[k] = jnp.sum(jnp.exp(scores - peak), axis=0, keepdims=True)
        return carry

    lax.fori_loop(0, lhs_slot.shape[0], one_slot, 0)


def slot_partials(lhs_slot, rhs_slot, lhs, rhs):
    slots = lhs_slot.shape[0]
    block_size = rhs.shape[2]
    part = jax.ShapeDtypeStruct((slots, 1, block_size), jnp.float32)
    smem = pl.BlockSpec(memory_space=pltpu.SMEM)
    vmem = pl.BlockSpec(memory_space=pltpu.VMEM)
    peak_parts, sum_parts = pl.pallas_call(
        slot_kernel,
        out_shape=(part, part),
        in_specs=[smem, smem, vmem, vmem],
        out_specs=(vmem, vmem),
        cost_estimate=pl.CostEstimate(
            flops=2 * slots * lhs.shape[1] * lhs.shape[2] * block_size,
            transcendentals=slots * lhs.shape[1] * block_size,
            bytes_accessed=(lhs.size + rhs.size) * 2 + 2 * slots * block_size * 4,
        ),
    )(lhs_slot, rhs_slot, lhs, rhs)
    return (peak_parts.reshape(slots, block_size), sum_parts.reshape(slots, block_size))


def bias_columns(bias):
    scaled = bias / ip_scale
    hi = lax.reduce_precision(scaled, exponent_bits=8, mantissa_bits=7)
    rest = scaled - hi
    mid = lax.reduce_precision(rest, exponent_bits=8, mantissa_bits=7)
    lo = rest - mid
    return jnp.stack([hi, mid, lo], axis=-1).astype(jnp.bfloat16)


def with_bias(points_t, bias):
    blocks, block_size, dim = points_t.shape
    pad = jnp.zeros((blocks, block_size, AUG - dim - 3), jnp.bfloat16)
    return jnp.concatenate([points_t, bias_columns(bias), pad], axis=-1)


def with_ones(points):
    blocks, dim, block_size = points.shape
    ones = jnp.ones((blocks, 3, block_size), jnp.bfloat16)
    pad = jnp.zeros((blocks, AUG - dim - 3, block_size), jnp.bfloat16)
    return jnp.concatenate([points, ones, pad], axis=1)


def block_combine(peak_parts, sum_parts, members, slot_block, usable):
    block_peak = jnp.max(jnp.where(members[:, :, None], peak_parts[None, :, :], neg_big), axis=1)
    scale = jnp.where(usable[:, None], jnp.exp(peak_parts - block_peak[slot_block]), 0.0)
    block_sum = jnp.dot(
        members.astype(jnp.float32), sum_parts * scale, precision=lax.Precision.HIGHEST
    )
    return (block_peak, block_sum)


def lse_allreduce(peak_vals, totals, axis):
    size = lax.axis_size(axis)
    if size & (size - 1):
        whole_peak = lax.pmax(peak_vals, axis)
        whole_sum = lax.psum(totals * jnp.exp(peak_vals - whole_peak), axis)
        return (whole_peak, whole_sum)
    here = lax.axis_index(axis)
    pair = jnp.stack([peak_vals, totals])
    step = 1
    while step < size:
        other = lax.ppermute(pair, axis, [(i, i ^ step) for i in range(size)])
        low_side = (here // step) % 2 == 0
        lo = jnp.where(low_side, pair, other)
        hi = jnp.where(low_side, other, pair)
        top = jnp.maximum(lo[0], hi[0])
        total = lo[1] * jnp.exp(lo[0] - top) + hi[1] * jnp.exp(hi[0] - top)
        pair = jnp.stack([top, total])
        step *= 2
    return (pair[0], pair[1])


def potential_from(peak_vals, totals, log_mass):
    return eps_reg * (log_mass - (peak_vals + jnp.log(totals)))


def body(row_points, col_points, block_lists):
    row_blocks_here = row_points.shape[0]
    col_blocks_here = col_points.shape[0]
    block_size = row_points.shape[2]
    row_mass = -math.log(lax.axis_size("row") * row_blocks_here * block_size)
    col_mass = -math.log(lax.axis_size("col") * col_blocks_here * block_size)
    row_norms = jnp.sum(jnp.square(row_points.astype(jnp.float32)), axis=1)
    col_norms = jnp.sum(jnp.square(col_points.astype(jnp.float32)), axis=1)
    owned = (block_lists // col_blocks_here == lax.axis_index("col")).reshape(-1)
    entry_rank = jnp.cumsum(owned.astype(jnp.int32)) - 1
    slot_list = jnp.arange(CAPACITY, dtype=jnp.int32)
    picked = owned[None, :] & (entry_rank[None, :] == slot_list[:, None])
    entries = jnp.arange(owned.shape[0], dtype=jnp.int32)
    entry_of_slot = jnp.sum(jnp.where(picked, entries[None, :], 0), axis=1)
    usable = jnp.any(picked, axis=1)
    row_slot = entry_of_slot // block_lists.shape[1]
    col_slot = block_lists.reshape(-1)[entry_of_slot] % col_blocks_here
    row_members = (row_slot[None, :] == jnp.arange(row_blocks_here)[:, None]) & usable[None, :]
    col_members = (col_slot[None, :] == jnp.arange(col_blocks_here)[:, None]) & usable[None, :]
    row_t = jnp.swapaxes(row_points, 1, 2)
    col_t = jnp.swapaxes(col_points, 1, 2)
    row_ones = with_ones(row_points)
    col_ones = with_ones(col_points)
    row_own = -row_norms / (DIM * eps_reg)
    col_own = -col_norms / (DIM * eps_reg)
    def sweep(step, carry):
        row_potential, col_potential = carry
        col_bias = (col_potential - col_norms / DIM) / eps_reg
        peak_parts, sum_parts = slot_partials(
            col_slot, row_slot, with_bias(col_t, col_bias), row_ones
        )
        block_peak, block_sum = block_combine(peak_parts, sum_parts, row_members, row_slot, usable)
        whole_peak, whole_sum = lse_allreduce(block_peak + row_own, block_sum, "col")
        row_potential = potential_from(whole_peak, whole_sum, row_mass)
        row_bias = (row_potential - row_norms / DIM) / eps_reg
        peak_parts, sum_parts = slot_partials(
            row_slot, col_slot, with_bias(row_t, row_bias), col_ones
        )
        block_peak, block_sum = block_combine(peak_parts, sum_parts, col_members, col_slot, usable)
        whole_peak, whole_sum = lse_allreduce(block_peak + col_own, block_sum, "row")
        col_potential = potential_from(whole_peak, whole_sum, col_mass)
        return (row_potential, col_potential)

    start = (
        jnp.zeros((row_blocks_here, block_size), jnp.float32),
        jnp.zeros((col_blocks_here, block_size), jnp.float32),
    )
    row_potential, col_potential = lax.fori_loop(0, ITERS, sweep, start)
    return (row_potential, col_potential)


def solution(mesh):
    placed = (P("row", None, None), P("col", None, None), P("row", None))
    return jax.shard_map(
        body,
        mesh=mesh,
        in_specs=placed,
        out_specs=(P("row", None), P("col", None)),
        check_vma=False,
    )
```

time: 480 us -> 688 us (1.43)
  Pallas kernels: 0 us -> 151 us
  other arithmetic: 32.2 us -> 137 us
  matrix products: 91.2 us -> 8.73 us
  local copies, waits for them, and re-layouts: 158 us -> 215 us
  waiting for transfers between devices: 88.6 us -> 69.2 us
    pallas_call x0 -> x8, Pallas kernels: none -> 151 us  [slot_partials(): pl.pallas_call(slot_kernel, out_shape=(part, part), in_specs=[smem, smem,...]
    gather x264 -> x0, local copies, waits for them, and re-layouts: 149 us -> none  [the longest x64 36.1 us: tile_partials(): row_tiles = row_points[row_index]]
    another operation x2 -> x18, other arithmetic: 0.31 us -> 120 us
    dot_general x64 -> x0, matrix products: 89.4 us -> none  [tile_partials(): jnp.einsum('sdp,sdq->spq', row_tiles, col_tiles, preferred_element_type=j...]
    concatenate x0 -> x10, local copies, waits for them, and re-layouts: none -> 88.3 us  [the longest x8 88.1 us: with_bias(): return jnp.concatenate([points_t, bias_columns(bias), pad], axis=-1)]
    squeeze x0 -> x20, local copies, waits for them, and re-layouts: none -> 74.1 us  [the longest x8 37.2 us: lse_allreduce(): total = lo[1] * jnp.exp(lo[0] - top) + hi[1] * jnp.exp(hi[0] - top)]
    ppermute x32, waiting for transfers between devices: 88.6 us -> 69.2 us  [lse_allreduce(): other = lax.ppermute(pair, axis, [(i, i ^ step) for i in range(size)])]
    reduce_sum x64 -> x0, other arithmetic: 18.8 us -> none  [tile_partials(): jnp.sum(jnp.exp(scores - jnp.expand_dims(peak_vals, reduce_axis)), axis=r...]
  transfers between devices with their start and end apart: 32 -> 32, of which waited for: 32 -> 30; matrix products, arithmetic and copies ran while one was open for 0% -> 3% of each run, Pallas kernels for 0% -> 0%
where the time goes in v2:
time: 688 us; the launch traced here: 682 us
  local copies, waits for them, and re-layouts  215 us (31%)
  Pallas kernels  151 us (22%)
  other arithmetic  137 us (20%)
  starting transfers between devices  99.1 us (14%)
  waiting for transfers between devices  69.2 us (10%)
  matrix products  8.73 us (1%)
    pallas_call x8, Pallas kernels, slot_partials(): pl.pallas_call(slot_kernel, out_shape=(part, part), in_specs=[smem, smem,...  151 us
    another operation x10, other arithmetic  120 us
    ppermute x32, starting transfers between devices, lse_allreduce(): other = lax.ppermute(pair, axis, [(i, i ^ step) for i in range(size)])  99.1 us
    concatenate x8, local copies, waits for them, and re-layouts, with_bias(): return jnp.concatenate([points_t, bias_columns(bias), pad], axis=-1)  88.1 us
    ppermute x32, waiting for transfers between devices, lse_allreduce(): other = lax.ppermute(pair, axis, [(i, i ^ step) for i in range(size)])  69.2 us
    squeeze x8, local copies, waits for them, and re-layouts, lse_allreduce(): total = lo[1] * jnp.exp(lo[0] - top) + hi[1] * jnp.exp(hi[0] - top)  37.2 us
    squeeze x12, local copies, waits for them, and re-layouts, lse_allreduce(): top = jnp.maximum(lo[0], hi[0])  36.9 us
    div x4, local copies, waits for them, and re-layouts, sweep(): row_bias = (row_potential - row_norms / DIM) / eps_reg  18.7 us
  transfers between devices with their start and end apart: 32, of which 30 were waited for; matrix products, arithmetic and copies ran while one was open for 3% of the time, Pallas kernels for 0%

profile of v2, /device:TPU:1, one launch (start us, length us, event | category | flops | bytes accessed | tf_op | source)
XLA Modules:
  0.0 681.8 jit_solution(8913503579332606546)
XLA Ops:
  15.1 666.1 %while.18 = (s32[]{:T(128)}, f32[64,256]{1,0:T(8,128)}, f32[4,256]{1,0:T(4,128)S(1)}, f32[4,256]{1,0:T(4,128)S(1)}, bf16[4,256,64]{2,1,0:T(8,128)(2,1)S(1)}, /*i...) while((s32[]{:T(128)}, f32[64,256]{1,0:T(8,128)}, ...), condition=%wide.region_9.10_spmd.clone.clone.clone, body=%wide.region_6.9_spmd.clone.clone.clone.sunk | while | flops 2164816384 | bytes 32302908 | solution.py:158
  17.3 18.9 %eval_jaxpr.10 = (f32[64,1,256]{2,1,0:T(1,128)}, f32[64,1,256]{2,1,0:T(1,128)}) custom-call(s32[64]{0:T(128)S(1)} %get-tuple-element.716.lhs_slot.rhs_slot, s32[64]{0:T(128)S(1)} %get-tuple-element.717.rhs_slot.lhs_slot, bf16[4,256,128]{2,1,0:T(8,128)(2,1)} %concatenate.24.lhs_ref, bf16[64,128,256]{2,1,0:T(8,128)(2,1)} %get-tuple-element.718.rhs_ref), custom_call_target="tpu_custom_call" | custom-call | flops 1073741824 | bytes 4587520 | tf_op jit(solution)/shard_map/while/body/eval_jaxpr/pallas_call | solution.py:41
  60.9 7.3 %collective-permute-start.4 = (f32[2,64,256]{2,1,0:T(8,128)S(1)}, f32[2,64,256]{2,1,0:T(8,128)S(1)}, u32[]{:S(2)}, u32[]{:S(2)}) collective-permute-start(f32[2,64,256]{2,1,0:T(8,128)S(1)} %pad_maximum_fusion.20), channel_id=1, source_target_pairs={{0,16},{1,17},{2,18},{3,19},{4,20},{5,21},{6,22},{7,23},{8,24},{9,... | collective-permute-start | bytes 393224 | tf_op jit(solution)/shard_map/while/body/eval_jaxpr/ppermute | solution.py:96
  68.2 4.7 copy.142
  73.0 4.7 copy.143
  77.7 4.6 copy.144
  82.3 4.6 copy.145
  86.9 4.6 copy.146
  91.5 21.0 %fusion.92 = (bf16[64,256,1]{2,1,0:T(8,128)(2,1)}, f32[64,256,1]{2,1,0:T(8,128)}) fusion(f32[64,256,1]{2,1,0:T(8,128)} %copy.142, f32[64,256,1]{2,1,0:T(8,128)} %copy.143, f32[64,256,1]{2,1,0:T(8,128)} %copy.144, f32[64,256,1]{2,1,0:T(8,128)} %copy.145, f32[64,256,1]{2,1,0:T(8,128)} %copy.146), kind=kLoop, calls=%fused_computation.9.clone.1 | loop fusion | flops 262144 | bytes 425984 | tf_op jit(solution)/shard_map/convert.2
  112.5 8.9 %reduce-precision_convert_fusion.5 = (bf16[64,256,1]{2,1,0:T(8,128)(2,1)}, bf16[64,256,1]{2,1,0:T(8,128)(2,1)}) fusion(f32[64,256,1]{2,1,0:T(8,128)} %get-tuple-element.643), kind=kLoop, calls=%fused_computation.6.clone.1 | loop fusion | flops 81920 | bytes 131072 | tf_op jit(solution)/shard_map/convert.1
  124.4 20.8 %concatenate.25.lhs_ref = bf16[64,256,128]{2,1,0:T(8,128)(2,1)} concatenate(bf16[64,256,64]{2,1,0:T(8,128)(2,1)} %get-tuple-element.722, bf16[64,256,1]{2,1,0:T(8,128)(2,1)} %get-tuple-element.644, bf16[64,256,1]{2,1,0:T(8,128)(2,1)} %get-tuple-element.645, bf16[64,256,1]{2,1,0:T(8,128)(2,1)} %get-tuple-element.646, bf16[64,256,61]{2,1,0:T(8,128)(2,1)} %broadcast.484), dimensions={2} | concatenate | bytes 8388608 | tf_op jit(solution)/shard_map/while/body/eval_jaxpr/concatenate | solution.py:67
  145.2 18.8 %eval_jaxpr.11 = (f32[64,1,256]{2,1,0:T(1,128)}, f32[64,1,256]{2,1,0:T(1,128)}) custom-call(s32[64]{0:T(128)S(1)} %get-tuple-element.717.rhs_slot.lhs_slot, s32[64]{0:T(128)S(1)} %get-tuple-element.716.lhs_slot.rhs_slot, bf16[64,256,128]{2,1,0:T(8,128)(2,1)} %concatenate.25.lhs_ref, bf16[4,128,256]{2,1,0:T(8,128)(2,1)S(1)} %get-tuple-element.723.rhs_ref), custom_call_target="tpu_custom_call" | custom-call | flops 1073741824 | bytes 4587520 | tf_op jit(solution)/shard_map/while/body/eval_jaxpr/pallas_call | solution.py:41
  166.7 6.8 collective-permute-start.5
  183.1 18.9 %eval_jaxpr.10 = (f32[64,1,256]{2,1,0:T(1,128)}, f32[64,1,256]{2,1,0:T(1,128)}) custom-call(s32[64]{0:T(128)S(1)} %get-tuple-element.716.lhs_slot.rhs_slot, s32[64]{0:T(128)S(1)} %get-tuple-element.717.rhs_slot.lhs_slot, bf16[4,256,128]{2,1,0:T(8,128)(2,1)} %concatenate.24.lhs_ref, bf16[64,128,256]{2,1,0:T(8,128)(2,1)} %get-tuple-element.718.rhs_ref), custom_call_target="tpu_custom_call" | custom-call | flops 1073741824 | bytes 4587520 | tf_op jit(solution)/shard_map/while/body/eval_jaxpr/pallas_call | solution.py:41
  221.3 5.5 collective-permute-done.3
  230.8 4.7 copy.142
  235.6 4.7 copy.143
  240.3 4.6 copy.144
  244.9 4.6 copy.145
  249.5 4.6 copy.146
  254.1 21.0 %fusion.92 = (bf16[64,256,1]{2,1,0:T(8,128)(2,1)}, f32[64,256,1]{2,1,0:T(8,128)}) fusion(f32[64,256,1]{2,1,0:T(8,128)} %copy.142, f32[64,256,1]{2,1,0:T(8,128)} %copy.143, f32[64,256,1]{2,1,0:T(8,128)} %copy.144, f32[64,256,1]{2,1,0:T(8,128)} %copy.145, f32[64,256,1]{2,1,0:T(8,128)} %copy.146), kind=kLoop, calls=%fused_computation.9.clone.1 | loop fusion | flops 262144 | bytes 425984 | tf_op jit(solution)/shard_map/convert.2
  275.1 8.9 %reduce-precision_convert_fusion.5 = (bf16[64,256,1]{2,1,0:T(8,128)(2,1)}, bf16[64,256,1]{2,1,0:T(8,128)(2,1)}) fusion(f32[64,256,1]{2,1,0:T(8,128)} %get-tuple-element.643), kind=kLoop, calls=%fused_computation.6.clone.1 | loop fusion | flops 81920 | bytes 131072 | tf_op jit(solution)/shard_map/convert.1
  287.0 20.8 %concatenate.25.lhs_ref = bf16[64,256,128]{2,1,0:T(8,128)(2,1)} concatenate(bf16[64,256,64]{2,1,0:T(8,128)(2,1)} %get-tuple-element.722, bf16[64,256,1]{2,1,0:T(8,128)(2,1)} %get-tuple-element.644, bf16[64,256,1]{2,1,0:T(8,128)(2,1)} %get-tuple-element.645, bf16[64,256,1]{2,1,0:T(8,128)(2,1)} %get-tuple-element.646, bf16[64,256,61]{2,1,0:T(8,128)(2,1)} %broadcast.484), dimensions={2} | concatenate | bytes 8388608 | tf_op jit(solution)/shard_map/while/body/eval_jaxpr/concatenate | solution.py:67
  307.8 18.8 %eval_jaxpr.11 = (f32[64,1,256]{2,1,0:T(1,128)}, f32[64,1,256]{2,1,0:T(1,128)}) custom-call(s32[64]{0:T(128)S(1)} %get-tuple-element.717.rhs_slot.lhs_slot, s32[64]{0:T(128)S(1)} %get-tuple-element.716.lhs_slot.rhs_slot, bf16[64,256,128]{2,1,0:T(8,128)(2,1)} %concatenate.25.lhs_ref, bf16[4,128,256]{2,1,0:T(8,128)(2,1)S(1)} %get-tuple-element.723.rhs_ref), custom_call_target="tpu_custom_call" | custom-call | flops 1073741824 | bytes 4587520 | tf_op jit(solution)/shard_map/while/body/eval_jaxpr/pallas_call | solution.py:41
  329.3 9.4 %collective-permute-start.5 = (f32[2,4,256]{2,1,0:T(4,128)S(1)}, f32[2,4,256]{2,1,0:T(4,128)S(1)}, u32[]{:S(2)}, u32[]{:S(2)}) collective-permute-start(f32[2,4,256]{2,1,0:T(4,128)S(1)} %pad_maximum_fusion.21), channel_id=1, source_target_pairs={{0,32},{32,0},{64,96},{96,64},{128,160},{160,128},{192,224},{224,1... | collective-permute-start | bytes 24584 | tf_op jit(solution)/shard_map/while/body/eval_jaxpr/ppermute | solution.py:96
  348.3 18.9 %eval_jaxpr.10 = (f32[64,1,256]{2,1,0:T(1,128)}, f32[64,1,256]{2,1,0:T(1,128)}) custom-call(s32[64]{0:T(128)S(1)} %get-tuple-element.716.lhs_slot.rhs_slot, s32[64]{0:T(128)S(1)} %get-tuple-element.717.rhs_slot.lhs_slot, bf16[4,256,128]{2,1,0:T(8,128)(2,1)} %concatenate.24.lhs_ref, bf16[64,128,256]{2,1,0:T(8,128)(2,1)} %get-tuple-element.718.rhs_ref), custom_call_target="tpu_custom_call" | custom-call | flops 1073741824 | bytes 4587520 | tf_op jit(solution)/shard_map/while/body/eval_jaxpr/pallas_call | solution.py:41
  388.0 5.5 collective-permute-done.3
  395.9 4.7 copy.142
  403.0 4.7 copy.143
  407.6 4.6 copy.144
  412.2 4.6 copy.145
  421.5 21.0 %fusion.92 = (bf16[64,256,1]{2,1,0:T(8,128)(2,1)}, f32[64,256,1]{2,1,0:T(8,128)}) fusion(f32[64,256,1]{2,1,0:T(8,128)} %copy.142, f32[64,256,1]{2,1,0:T(8,128)} %copy.143, f32[64,256,1]{2,1,0:T(8,128)} %copy.144, f32[64,256,1]{2,1,0:T(8,128)} %copy.145, f32[64,256,1]{2,1,0:T(8,128)} %copy.146), kind=kLoop, calls=%fused_computation.9.clone.1 | loop fusion | flops 262144 | bytes 425984 | tf_op jit(solution)/shard_map/convert.2
  442.5 8.9 %reduce-precision_convert_fusion.5 = (bf16[64,256,1]{2,1,0:T(8,128)(2,1)}, bf16[64,256,1]{2,1,0:T(8,128)(2,1)}) fusion(f32[64,256,1]{2,1,0:T(8,128)} %get-tuple-element.643), kind=kLoop, calls=%fused_computation.6.clone.1 | loop fusion | flops 81920 | bytes 131072 | tf_op jit(solution)/shard_map/convert.1
  454.4 20.8 %concatenate.25.lhs_ref = bf16[64,256,128]{2,1,0:T(8,128)(2,1)} concatenate(bf16[64,256,64]{2,1,0:T(8,128)(2,1)} %get-tuple-element.722, bf16[64,256,1]{2,1,0:T(8,128)(2,1)} %get-tuple-element.644, bf16[64,256,1]{2,1,0:T(8,128)(2,1)} %get-tuple-element.645, bf16[64,256,1]{2,1,0:T(8,128)(2,1)} %get-tuple-element.646, bf16[64,256,61]{2,1,0:T(8,128)(2,1)} %broadcast.484), dimensions={2} | concatenate | bytes 8388608 | tf_op jit(solution)/shard_map/while/body/eval_jaxpr/concatenate | solution.py:67
  475.1 18.8 %eval_jaxpr.11 = (f32[64,1,256]{2,1,0:T(1,128)}, f32[64,1,256]{2,1,0:T(1,128)}) custom-call(s32[64]{0:T(128)S(1)} %get-tuple-element.717.rhs_slot.lhs_slot, s32[64]{0:T(128)S(1)} %get-tuple-element.716.lhs_slot.rhs_slot, bf16[64,256,128]{2,1,0:T(8,128)(2,1)} %concatenate.25.lhs_ref, bf16[4,128,256]{2,1,0:T(8,128)(2,1)S(1)} %get-tuple-element.723.rhs_ref), custom_call_target="tpu_custom_call" | custom-call | flops 1073741824 | bytes 4587520 | tf_op jit(solution)/shard_map/while/body/eval_jaxpr/pallas_call | solution.py:41
  496.7 10.1 %collective-permute-start.5 = (f32[2,4,256]{2,1,0:T(4,128)S(1)}, f32[2,4,256]{2,1,0:T(4,128)S(1)}, u32[]{:S(2)}, u32[]{:S(2)}) collective-permute-start(f32[2,4,256]{2,1,0:T(4,128)S(1)} %pad_maximum_fusion.21), channel_id=1, source_target_pairs={{0,32},{32,0},{64,96},{96,64},{128,160},{160,128},{192,224},{224,1... | collective-permute-start | bytes 24584 | tf_op jit(solution)/shard_map/while/body/eval_jaxpr/ppermute | solution.py:96
  516.4 18.9 %eval_jaxpr.10 = (f32[64,1,256]{2,1,0:T(1,128)}, f32[64,1,256]{2,1,0:T(1,128)}) custom-call(s32[64]{0:T(128)S(1)} %get-tuple-element.716.lhs_slot.rhs_slot, s32[64]{0:T(128)S(1)} %get-tuple-element.717.rhs_slot.lhs_slot, bf16[4,256,128]{2,1,0:T(8,128)(2,1)} %concatenate.24.lhs_ref, bf16[64,128,256]{2,1,0:T(8,128)(2,1)} %get-tuple-element.718.rhs_ref), custom_call_target="tpu_custom_call" | custom-call | flops 1073741824 | bytes 4587520 | tf_op jit(solution)/shard_map/while/body/eval_jaxpr/pallas_call | solution.py:41
  554.7 5.5 collective-permute-done.3
  563.4 4.7 copy.142
  569.1 4.7 copy.143
  573.8 4.6 copy.144
  578.4 4.6 copy.145
  583.1 4.6 copy.146
  587.7 21.0 %fusion.92 = (bf16[64,256,1]{2,1,0:T(8,128)(2,1)}, f32[64,256,1]{2,1,0:T(8,128)}) fusion(f32[64,256,1]{2,1,0:T(8,128)} %copy.142, f32[64,256,1]{2,1,0:T(8,128)} %copy.143, f32[64,256,1]{2,1,0:T(8,128)} %copy.144, f32[64,256,1]{2,1,0:T(8,128)} %copy.145, f32[64,256,1]{2,1,0:T(8,128)} %copy.146), kind=kLoop, calls=%fused_computation.9.clone.1 | loop fusion | flops 262144 | bytes 425984 | tf_op jit(solution)/shard_map/convert.2
  608.6 8.9 %reduce-precision_convert_fusion.5 = (bf16[64,256,1]{2,1,0:T(8,128)(2,1)}, bf16[64,256,1]{2,1,0:T(8,128)(2,1)}) fusion(f32[64,256,1]{2,1,0:T(8,128)} %get-tuple-element.643), kind=kLoop, calls=%fused_computation.6.clone.1 | loop fusion | flops 81920 | bytes 131072 | tf_op jit(solution)/shard_map/convert.1
  620.5 20.8 %concatenate.25.lhs_ref = bf16[64,256,128]{2,1,0:T(8,128)(2,1)} concatenate(bf16[64,256,64]{2,1,0:T(8,128)(2,1)} %get-tuple-element.722, bf16[64,256,1]{2,1,0:T(8,128)(2,1)} %get-tuple-element.644, bf16[64,256,1]{2,1,0:T(8,128)(2,1)} %get-tuple-element.645, bf16[64,256,1]{2,1,0:T(8,128)(2,1)} %get-tuple-element.646, bf16[64,256,61]{2,1,0:T(8,128)(2,1)} %broadcast.484), dimensions={2} | concatenate | bytes 8388608 | tf_op jit(solution)/shard_map/while/body/eval_jaxpr/concatenate | solution.py:67
  641.3 18.8 %eval_jaxpr.11 = (f32[64,1,256]{2,1,0:T(1,128)}, f32[64,1,256]{2,1,0:T(1,128)}) custom-call(s32[64]{0:T(128)S(1)} %get-tuple-element.717.rhs_slot.lhs_slot, s32[64]{0:T(128)S(1)} %get-tuple-element.716.lhs_slot.rhs_slot, bf16[64,256,128]{2,1,0:T(8,128)(2,1)} %concatenate.25.lhs_ref, bf16[4,128,256]{2,1,0:T(8,128)(2,1)S(1)} %get-tuple-element.723.rhs_ref), custom_call_target="tpu_custom_call" | custom-call | flops 1073741824 | bytes 4587520 | tf_op jit(solution)/shard_map/while/body/eval_jaxpr/pallas_call | solution.py:41
  662.9 10.7 %collective-permute-start.5 = (f32[2,4,256]{2,1,0:T(4,128)S(1)}, f32[2,4,256]{2,1,0:T(4,128)S(1)}, u32[]{:S(2)}, u32[]{:S(2)}) collective-permute-start(f32[2,4,256]{2,1,0:T(4,128)S(1)} %pad_maximum_fusion.21), channel_id=1, source_target_pairs={{0,32},{32,0},{64,96},{96,64},{128,160},{160,128},{192,224},{224,1... | collective-permute-start | bytes 24584 | tf_op jit(solution)/shard_map/while/body/eval_jaxpr/ppermute | solution.py:96
  (295 shorter events, 177.1 us)
Async XLA Ops:
  0.6 14.4 %copy-start.1 = (bf16[4,64,256]{2,1,0:T(8,128)(2,1)S(1)}, bf16[4,64,256]{2,1,0:T(8,128)(2,1)}, u32[]{:S(2)}) copy-start(bf16[4,64,256]{2,1,0:T(8,128)(2,1)} %param.6) | copy-start | bytes 393220
  0.6 10.3 %copy-start = (bf16[64,64,256]{2,1,0:T(8,128)(2,1)S(1)}, bf16[64,64,256]{2,1,0:T(8,128)(2,1)}, u32[]{:S(2)}) copy-start(bf16[64,64,256]{2,1,0:T(8,128)(2,1)} %param.5) | copy-start | bytes 6291460
  40.1 4.6 collective-permute-start
  44.7 6.1 collective-permute-start.1
  50.9 4.1 collective-permute-start.2
  55.1 5.7 collective-permute-start.3
  60.9 12.0 %collective-permute-start.4 = (f32[2,64,256]{2,1,0:T(8,128)S(1)}, f32[2,64,256]{2,1,0:T(8,128)S(1)}, u32[]{:S(2)}, u32[]{:S(2)}) collective-permute-start(f32[2,64,256]{2,1,0:T(8,128)S(1)} %pad_maximum_fusion.20), channel_id=1, source_target_pairs={{0,16},{1,17},{2,18},{3,19},{4,20},{5,21},{6,22},{7,23},{8,24},{9,... | collective-permute-start | bytes 393224 | tf_op jit(solution)/shard_map/while/body/eval_jaxpr/ppermute | solution.py:96
  166.7 7.6 %collective-permute-start.5 = (f32[2,4,256]{2,1,0:T(4,128)S(1)}, f32[2,4,256]{2,1,0:T(4,128)S(1)}, u32[]{:S(2)}, u32[]{:S(2)}) collective-permute-start(f32[2,4,256]{2,1,0:T(4,128)S(1)} %pad_maximum_fusion.21), channel_id=1, source_target_pairs={{0,32},{32,0},{64,96},{96,64},{128,160},{160,128},{192,224},{224,1... | collective-permute-start | bytes 24584 | tf_op jit(solution)/shard_map/while/body/eval_jaxpr/ppermute | solution.py:96
  174.3 2.6 collective-permute-start.6
  177.0 4.1 collective-permute-start.7
  205.9 3.9 collective-permute-start
  209.9 6.7 collective-permute-start.1
  216.7 3.9 collective-permute-start.2
  220.7 6.1 collective-permute-start.3
  226.8 8.7 %collective-permute-start.4 = (f32[2,64,256]{2,1,0:T(8,128)S(1)}, f32[2,64,256]{2,1,0:T(8,128)S(1)}, u32[]{:S(2)}, u32[]{:S(2)}) collective-permute-start(f32[2,64,256]{2,1,0:T(8,128)S(1)} %pad_maximum_fusion.20), channel_id=1, source_target_pairs={{0,16},{1,17},{2,18},{3,19},{4,20},{5,21},{6,22},{7,23},{8,24},{9,... | collective-permute-start | bytes 393224 | tf_op jit(solution)/shard_map/while/body/eval_jaxpr/ppermute | solution.py:96
  329.3 10.2 %collective-permute-start.5 = (f32[2,4,256]{2,1,0:T(4,128)S(1)}, f32[2,4,256]{2,1,0:T(4,128)S(1)}, u32[]{:S(2)}, u32[]{:S(2)}) collective-permute-start(f32[2,4,256]{2,1,0:T(4,128)S(1)} %pad_maximum_fusion.21), channel_id=1, source_target_pairs={{0,32},{32,0},{64,96},{96,64},{128,160},{160,128},{192,224},{224,1... | collective-permute-start | bytes 24584 | tf_op jit(solution)/shard_map/while/body/eval_jaxpr/ppermute | solution.py:96
  339.6 2.6 collective-permute-start.6
  342.2 4.1 collective-permute-start.7
  371.1 5.4 collective-permute-start
  376.6 6.7 collective-permute-start.1
  383.4 3.9 collective-permute-start.2
  387.4 6.1 collective-permute-start.3
  393.6 9.3 %collective-permute-start.4 = (f32[2,64,256]{2,1,0:T(8,128)S(1)}, f32[2,64,256]{2,1,0:T(8,128)S(1)}, u32[]{:S(2)}, u32[]{:S(2)}) collective-permute-start(f32[2,64,256]{2,1,0:T(8,128)S(1)} %pad_maximum_fusion.20), channel_id=1, source_target_pairs={{0,16},{1,17},{2,18},{3,19},{4,20},{5,21},{6,22},{7,23},{8,24},{9,... | collective-permute-start | bytes 393224 | tf_op jit(solution)/shard_map/while/body/eval_jaxpr/ppermute | solution.py:96
  496.7 10.9 %collective-permute-start.5 = (f32[2,4,256]{2,1,0:T(4,128)S(1)}, f32[2,4,256]{2,1,0:T(4,128)S(1)}, u32[]{:S(2)}, u32[]{:S(2)}) collective-permute-start(f32[2,4,256]{2,1,0:T(4,128)S(1)} %pad_maximum_fusion.21), channel_id=1, source_target_pairs={{0,32},{32,0},{64,96},{96,64},{128,160},{160,128},{192,224},{224,1... | collective-permute-start | bytes 24584 | tf_op jit(solution)/shard_map/while/body/eval_jaxpr/ppermute | solution.py:96
  507.6 2.6 collective-permute-start.6
  510.3 4.1 collective-permute-start.7
  539.2 3.9 collective-permute-start
  543.2 6.9 %collective-permute-start.1 = (f32[2,64,256]{2,1,0:T(8,128)S(1)}, f32[2,64,256]{2,1,0:T(8,128)S(1)}, u32[]{:S(2)}, u32[]{:S(2)}) collective-permute-start(f32[2,64,256]{2,1,0:T(8,128)S(1)} %pad_maximum_fusion.17), channel_id=1, source_target_pairs={{0,2},{1,3},{2,0},{3,1},{4,6},{5,7},{6,4},{7,5},{8,10},{9,11},{10,... | collective-permute-start | bytes 393224 | tf_op jit(solution)/shard_map/while/body/eval_jaxpr/ppermute | solution.py:96
  550.2 3.9 collective-permute-start.2
  554.2 6.1 collective-permute-start.3
  560.3 8.8 %collective-permute-start.4 = (f32[2,64,256]{2,1,0:T(8,128)S(1)}, f32[2,64,256]{2,1,0:T(8,128)S(1)}, u32[]{:S(2)}, u32[]{:S(2)}) collective-permute-start(f32[2,64,256]{2,1,0:T(8,128)S(1)} %pad_maximum_fusion.20), channel_id=1, source_target_pairs={{0,16},{1,17},{2,18},{3,19},{4,20},{5,21},{6,22},{7,23},{8,24},{9,... | collective-permute-start | bytes 393224 | tf_op jit(solution)/shard_map/while/body/eval_jaxpr/ppermute | solution.py:96
  662.9 11.5 %collective-permute-start.5 = (f32[2,4,256]{2,1,0:T(4,128)S(1)}, f32[2,4,256]{2,1,0:T(4,128)S(1)}, u32[]{:S(2)}, u32[]{:S(2)}) collective-permute-start(f32[2,4,256]{2,1,0:T(4,128)S(1)} %pad_maximum_fusion.21), channel_id=1, source_target_pairs={{0,32},{32,0},{64,96},{96,64},{128,160},{160,128},{192,224},{224,1... | collective-permute-start | bytes 24584 | tf_op jit(solution)/shard_map/while/body/eval_jaxpr/ppermute | solution.py:96
  674.4 2.6 collective-permute-start.6
  677.1 4.1 collective-permute-start.7
  681.2 0.6 copy-start.2

commit v3 on v2

--- a/solution.py
+++ b/solution.py
@@ -10,7 +10,7 @@
 DIM = 64
 ITERS = 4
 CAPACITY = 64
-AUG = 128
+LANES = 128
 
 
 eps_reg = 0.05
@@ -18,12 +18,22 @@
 ip_scale = 2.0 / (DIM * eps_reg)
 
 
-def slot_kernel(lhs_slot, rhs_slot, lhs_ref, rhs_ref, peak_ref, sum_ref):
+def slot_kernel(lhs_slot, rhs_slot, lhs_ref, rhs_ref, bias_ref, peak_ref, sum_ref, spread_ref):
+    lanes = spread_ref.shape[2]
+
+    def spread(block, carry):
+        row = jnp.broadcast_to(bias_ref[block], (lanes, bias_ref.shape[2]))
+        spread_ref[block] = jnp.transpose(row)
+        return carry
+
+    lax.fori_loop(0, spread_ref.shape[0], spread, 0)
+
     def one_slot(k, carry):
-        tile = jnp.dot(
-            lhs_ref[lhs_slot[k]], rhs_ref[rhs_slot[k]], preferred_element_type=jnp.float32
-        )
-        scores = tile * ip_scale
+        a = lhs_slot[k]
+        tile = jnp.dot(lhs_ref[a], rhs_ref[rhs_slot[k]], preferred_element_type=jnp.float32)
+        bias = spread_ref[a]
+        bias = jnp.concatenate([bias] * (tile.shape[1] // lanes), axis=1)
+        scores = tile * ip_scale + bias
         peak = jnp.max(scores, axis=0, keepdims=True)
         peak_ref[k] = peak
         sum_ref[k] = jnp.sum(jnp.exp(scores - peak), axis=0, keepdims=True)
@@ -32,46 +42,25 @@
     lax.fori_loop(0, lhs_slot.shape[0], one_slot, 0)
 
 
-def slot_partials(lhs_slot, rhs_slot, lhs, rhs):
+def slot_partials(lhs_slot, rhs_slot, lhs, rhs, bias):
     slots = lhs_slot.shape[0]
-    block_size = rhs.shape[2]
-    part = jax.ShapeDtypeStruct((slots, 1, block_size), jnp.float32)
+    blocks, block_size, dim = lhs.shape
+    part = jax.ShapeDtypeStruct((slots, 1, rhs.shape[2]), jnp.float32)
     smem = pl.BlockSpec(memory_space=pltpu.SMEM)
     vmem = pl.BlockSpec(memory_space=pltpu.VMEM)
     peak_parts, sum_parts = pl.pallas_call(
         slot_kernel,
         out_shape=(part, part),
-        in_specs=[smem, smem, vmem, vmem],
+        in_specs=[smem, smem, vmem, vmem, vmem],
         out_specs=(vmem, vmem),
+        scratch_shapes=[pltpu.VMEM((blocks, block_size, LANES), jnp.float32)],
         cost_estimate=pl.CostEstimate(
-            flops=2 * slots * lhs.shape[1] * lhs.shape[2] * block_size,
-            transcendentals=slots * lhs.shape[1] * block_size,
-            bytes_accessed=(lhs.size + rhs.size) * 2 + 2 * slots * block_size * 4,
+            flops=2 * slots * block_size * dim * rhs.shape[2],
+            transcendentals=slots * block_size * rhs.shape[2],
+            bytes_accessed=(lhs.size + rhs.size) * 2 + 2 * slots * rhs.shape[2] * 4,
         ),
-    )(lhs_slot, rhs_slot, lhs, rhs)
-    return (peak_parts.reshape(slots, block_size), sum_parts.reshape(slots, block_size))
-
-
-def bias_columns(bias):
-    scaled = bias / ip_scale
-    hi = lax.reduce_precision(scaled, exponent_bits=8, mantissa_bits=7)
-    rest = scaled - hi
-    mid = lax.reduce_precision(rest, exponent_bits=8, mantissa_bits=7)
-    lo = rest - mid
-    return jnp.stack([hi, mid, lo], axis=-1).astype(jnp.bfloat16)
-
-
-def with_bias(points_t, bias):
-    blocks, block_size, dim = points_t.shape
-    pad = jnp.zeros((blocks, block_size, AUG - dim - 3), jnp.bfloat16)
-    return jnp.concatenate([points_t, bias_columns(bias), pad], axis=-1)
-
-
-def with_ones(points):
-    blocks, dim, block_size = points.shape
-    ones = jnp.ones((blocks, 3, block_size), jnp.bfloat16)
-    pad = jnp.zeros((blocks, AUG - dim - 3, block_size), jnp.bfloat16)
-    return jnp.concatenate([points, ones, pad], axis=1)
+    )(lhs_slot, rhs_slot, lhs, rhs, bias.reshape(blocks, 1, block_size))
+    return (peak_parts.reshape(slots, -1), sum_parts.reshape(slots, -1))
 
 
 def block_combine(peak_parts, sum_parts, members, slot_block, usable):
@@ -129,22 +118,20 @@
     col_members = (col_slot[None, :] == jnp.arange(col_blocks_here)[:, None]) & usable[None, :]
     row_t = jnp.swapaxes(row_points, 1, 2)
     col_t = jnp.swapaxes(col_points, 1, 2)
-    row_ones = with_ones(row_points)
-    col_ones = with_ones(col_points)
     row_own = -row_norms / (DIM * eps_reg)
     col_own = -col_norms / (DIM * eps_reg)
     def sweep(step, carry):
         row_potential, col_potential = carry
         col_bias = (col_potential - col_norms / DIM) / eps_reg
         peak_parts, sum_parts = slot_partials(
-            col_slot, row_slot, with_bias(col_t, col_bias), row_ones
+            col_slot, row_slot, col_t, row_points, col_bias
         )
         block_peak, block_sum = block_combine(peak_parts, sum_parts, row_members, row_slot, usable)
         whole_peak, whole_sum = lse_allreduce(block_peak + row_own, block_sum, "col")
         row_potential = potential_from(whole_peak, whole_sum, row_mass)
         row_bias = (row_potential - row_norms / DIM) / eps_reg
         peak_parts, sum_parts = slot_partials(
-            row_slot, col_slot, with_bias(row_t, row_bias), col_ones
+            row_slot, col_slot, row_t, col_points, row_bias
         )
         block_peak, block_sum = block_combine(peak_parts, sum_parts, col_members, col_slot, usable)
         whole_peak, whole_sum = lse_allreduce(block_peak + col_own, block_sum, "row")

time: 688 us -> 406 us (0.59)
  local copies, waits for them, and re-layouts: 215 us -> 20.5 us
  other arithmetic: 137 us -> 18.4 us
  Pallas kernels: 151 us -> 168 us
  waiting for transfers between devices: 69.2 us -> 82.4 us
    another operation x18 -> x2, other arithmetic: 120 us -> 0.31 us
    concatenate x10 -> x0, local copies, waits for them, and re-layouts: 88.3 us -> none  [the longest x8 88.1 us: with_bias(): return jnp.concatenate([points_t, bias_columns(bias), pad], axis=-1)]
    squeeze x8 -> x0, local copies, waits for them, and re-layouts: 37.2 us -> none  [lse_allreduce(): total = lo[1] * jnp.exp(lo[0] - top) + hi[1] * jnp.exp(hi[0] - top)]
    squeeze x12 -> x4, local copies, waits for them, and re-layouts: 36.9 us -> 0.08 us  [lse_allreduce(): top = jnp.maximum(lo[0], hi[0])]
    div x4 -> x0, local copies, waits for them, and re-layouts: 18.7 us -> none  [sweep(): row_bias = (row_potential - row_norms / DIM) / eps_reg]
    pallas_call x8, Pallas kernels: 151 us -> 168 us  [slot_partials(): pl.pallas_call(slot_kernel, out_shape=(part, part), in_specs=[smem, smem,...]
    another operation x21 -> x1, local copies, waits for them, and re-layouts: 14.6 us -> 0.12 us
    ppermute x32, waiting for transfers between devices: 69.2 us -> 82.4 us  [lse_allreduce(): other = lax.ppermute(pair, axis, [(i, i ^ step) for i in range(size)])]
  transfers between devices with their start and end apart: 32 -> 32, of which waited for: 30 -> 32; matrix products, arithmetic and copies ran while one was open for 3% -> 1% of each run, Pallas kernels for 0% -> 0%
where the time goes in v3:
time: 406 us; the launch traced here: 402 us
  Pallas kernels  168 us (41%)
  starting transfers between devices  102 us (25%)
  waiting for transfers between devices  82.4 us (20%)
  local copies, waits for them, and re-layouts  20.5 us (5%)
  other arithmetic  18.4 us (5%)
  matrix products  8.72 us (2%)
    pallas_call x8, Pallas kernels, slot_partials(): pl.pallas_call(slot_kernel, out_shape=(part, part), in_specs=[smem, smem,...  168 us
    ppermute x32, starting transfers between devices, lse_allreduce(): other = lax.ppermute(pair, axis, [(i, i ^ step) for i in range(size)])  102 us
    ppermute x32, waiting for transfers between devices, lse_allreduce(): other = lax.ppermute(pair, axis, [(i, i ^ step) for i in range(size)])  82.4 us
    dot_general x8, matrix products, block_combine(): jnp.dot(members.astype(jnp.float32), sum_parts * scale, precision=lax.Pre...  8.72 us
  transfers between devices with their start and end apart: 32, of which 32 were waited for; matrix products, arithmetic and copies ran while one was open for 1% of the time, Pallas kernels for 0%

profile of v3, /device:TPU:1, one launch (start us, length us, event | category | flops | bytes accessed | tf_op | source)
XLA Modules:
  0.0 402.1 jit_solution(16992117402776653747)
XLA Ops:
  7.7 3.2 copy.46
  11.0 390.5 %while.18 = (s32[]{:T(128)}, f32[64,256]{1,0:T(8,128)}, f32[4,256]{1,0:T(4,128)S(1)}, f32[4,256]{1,0:T(4,128)S(1)}, s32[64]{0:T(128)S(1)}, /*index=5*/s32[64]{0:...) while((s32[]{:T(128)}, f32[64,256]{1,0:T(8,128)}, ...), condition=%wide.region_9.10_spmd.clone.clone.clone, body=%wide.region_6.9_spmd.clone.clone.clone.sunk | while | flops 1090900480 | bytes 15976267 | solution.py:145
  11.7 17.3 %eval_jaxpr.10 = (f32[64,1,256]{2,1,0:T(1,128)}, f32[64,1,256]{2,1,0:T(1,128)}) custom-call(s32[64]{0:T(128)S(1)} %get-tuple-element.681.lhs_slot.rhs_slot, s32[64]{0:T(128)S(1)} %get-tuple-element.682.rhs_slot.lhs_slot, bf16[4,256,64]{2,1,0:T(8,128)(2,1)S(1)} %get-tuple-element.683.lhs_ref, bf16[64,64,256]{2,1,0:T(8,128)(2,1)S(1)} %get-tuple-element.684.rhs_ref, ...), custom_call_target="tpu_custom_call" | custom-call | flops 536870912 | bytes 2359296 | tf_op jit(solution)/shard_map/while/body/eval_jaxpr/pallas_call | solution.py:51
  35.1 2.4 collective-permute-done
  37.5 3.7 collective-permute-start.1
  41.3 2.4 collective-permute-done.1
  45.5 2.4 collective-permute-done.2
  47.9 3.1 collective-permute-start.3
  51.0 2.7 collective-permute-done.3
  53.8 7.3 %collective-permute-start.4 = (f32[2,64,256]{2,1,0:T(8,128)S(1)}, f32[2,64,256]{2,1,0:T(8,128)S(1)}, u32[]{:S(2)}, u32[]{:S(2)}) collective-permute-start(f32[2,64,256]{2,1,0:T(8,128)S(1)} %pad_maximum_fusion.20), channel_id=1, source_target_pairs={{0,16},{1,17},{2,18},{3,19},{4,20},{5,21},{6,22},{7,23},{8,24},{9,... | collective-permute-start | bytes 393224 | tf_op jit(solution)/shard_map/while/body/eval_jaxpr/ppermute | solution.py:85
  61.0 3.2 collective-permute-done.4
  65.2 24.7 %eval_jaxpr.11 = (f32[64,1,256]{2,1,0:T(1,128)}, f32[64,1,256]{2,1,0:T(1,128)}) custom-call(s32[64]{0:T(128)S(1)} %get-tuple-element.682.rhs_slot.lhs_slot, s32[64]{0:T(128)S(1)} %get-tuple-element.681.lhs_slot.rhs_slot, bf16[64,256,64]{2,1,0:T(8,128)(2,1)} %get-tuple-element.688.lhs_ref, bf16[4,64,256]{2,1,0:T(8,128)(2,1)S(1)} %get-tuple-element.689.rhs_ref, ...), custom_call_target="tpu_custom_call" | custom-call | flops 536870912 | bytes 2359296 | tf_op jit(solution)/shard_map/while/body/eval_jaxpr/pallas_call | solution.py:51
  92.7 6.5 %collective-permute-start.5 = (f32[2,4,256]{2,1,0:T(4,128)S(1)}, f32[2,4,256]{2,1,0:T(4,128)S(1)}, u32[]{:S(2)}, u32[]{:S(2)}) collective-permute-start(f32[2,4,256]{2,1,0:T(4,128)S(1)} %pad_maximum_fusion.21), channel_id=1, source_target_pairs={{0,32},{32,0},{64,96},{96,64},{128,160},{160,128},{192,224},{224,1... | collective-permute-start | bytes 24584 | tf_op jit(solution)/shard_map/while/body/eval_jaxpr/ppermute | solution.py:85
  102.7 2.8 collective-permute-start.7
  107.5 17.4 %eval_jaxpr.10 = (f32[64,1,256]{2,1,0:T(1,128)}, f32[64,1,256]{2,1,0:T(1,128)}) custom-call(s32[64]{0:T(128)S(1)} %get-tuple-element.681.lhs_slot.rhs_slot, s32[64]{0:T(128)S(1)} %get-tuple-element.682.rhs_slot.lhs_slot, bf16[4,256,64]{2,1,0:T(8,128)(2,1)S(1)} %get-tuple-element.683.lhs_ref, bf16[64,64,256]{2,1,0:T(8,128)(2,1)S(1)} %get-tuple-element.684.rhs_ref, ...), custom_call_target="tpu_custom_call" | custom-call | flops 536870912 | bytes 2359296 | tf_op jit(solution)/shard_map/while/body/eval_jaxpr/pallas_call | solution.py:51
  130.1 2.5 collective-permute-done
  132.7 3.0 collective-permute-start.1
  135.7 3.8 collective-permute-done.1
  139.6 3.8 collective-permute-done.2
  144.1 5.5 %collective-permute-done.3 = f32[2,64,256]{2,1,0:T(8,128)S(1)} collective-permute-done((f32[2,64,256]{2,1,0:T(8,128)S(1)}, f32[2,64,256]{2,1,0:T(8,128)S(1)}, u32[]{:S(2)}, u32[]{:S(2)}) %collective-permute-start.3) | collective-permute-done | bytes 131104 | tf_op jit(solution)/shard_map/while/body/eval_jaxpr/ppermute | solution.py:85
  149.7 5.7 %collective-permute-start.4 = (f32[2,64,256]{2,1,0:T(8,128)S(1)}, f32[2,64,256]{2,1,0:T(8,128)S(1)}, u32[]{:S(2)}, u32[]{:S(2)}) collective-permute-start(f32[2,64,256]{2,1,0:T(8,128)S(1)} %pad_maximum_fusion.20), channel_id=1, source_target_pairs={{0,16},{1,17},{2,18},{3,19},{4,20},{5,21},{6,22},{7,23},{8,24},{9,... | collective-permute-start | bytes 393224 | tf_op jit(solution)/shard_map/while/body/eval_jaxpr/ppermute | solution.py:85
  155.4 3.8 collective-permute-done.4
  160.3 24.7 %eval_jaxpr.11 = (f32[64,1,256]{2,1,0:T(1,128)}, f32[64,1,256]{2,1,0:T(1,128)}) custom-call(s32[64]{0:T(128)S(1)} %get-tuple-element.682.rhs_slot.lhs_slot, s32[64]{0:T(128)S(1)} %get-tuple-element.681.lhs_slot.rhs_slot, bf16[64,256,64]{2,1,0:T(8,128)(2,1)} %get-tuple-element.688.lhs_ref, bf16[4,64,256]{2,1,0:T(8,128)(2,1)S(1)} %get-tuple-element.689.rhs_ref, ...), custom_call_target="tpu_custom_call" | custom-call | flops 536870912 | bytes 2359296 | tf_op jit(solution)/shard_map/while/body/eval_jaxpr/pallas_call | solution.py:51
  187.7 8.5 %collective-permute-start.5 = (f32[2,4,256]{2,1,0:T(4,128)S(1)}, f32[2,4,256]{2,1,0:T(4,128)S(1)}, u32[]{:S(2)}, u32[]{:S(2)}) collective-permute-start(f32[2,4,256]{2,1,0:T(4,128)S(1)} %pad_maximum_fusion.21), channel_id=1, source_target_pairs={{0,32},{32,0},{64,96},{96,64},{128,160},{160,128},{192,224},{224,1... | collective-permute-start | bytes 24584 | tf_op jit(solution)/shard_map/while/body/eval_jaxpr/ppermute | solution.py:85
  199.7 2.8 collective-permute-start.7
  204.5 17.3 %eval_jaxpr.10 = (f32[64,1,256]{2,1,0:T(1,128)}, f32[64,1,256]{2,1,0:T(1,128)}) custom-call(s32[64]{0:T(128)S(1)} %get-tuple-element.681.lhs_slot.rhs_slot, s32[64]{0:T(128)S(1)} %get-tuple-element.682.rhs_slot.lhs_slot, bf16[4,256,64]{2,1,0:T(8,128)(2,1)S(1)} %get-tuple-element.683.lhs_ref, bf16[64,64,256]{2,1,0:T(8,128)(2,1)S(1)} %get-tuple-element.684.rhs_ref, ...), custom_call_target="tpu_custom_call" | custom-call | flops 536870912 | bytes 2359296 | tf_op jit(solution)/shard_map/while/body/eval_jaxpr/pallas_call | solution.py:51
  227.5 2.4 collective-permute-done
  229.9 3.4 collective-permute-start.1
  233.3 3.2 collective-permute-done.1
  236.7 3.8 collective-permute-done.2
  241.2 5.5 %collective-permute-done.3 = f32[2,64,256]{2,1,0:T(8,128)S(1)} collective-permute-done((f32[2,64,256]{2,1,0:T(8,128)S(1)}, f32[2,64,256]{2,1,0:T(8,128)S(1)}, u32[]{:S(2)}, u32[]{:S(2)}) %collective-permute-start.3) | collective-permute-done | bytes 131104 | tf_op jit(solution)/shard_map/while/body/eval_jaxpr/ppermute | solution.py:85
  246.8 5.6 %collective-permute-start.4 = (f32[2,64,256]{2,1,0:T(8,128)S(1)}, f32[2,64,256]{2,1,0:T(8,128)S(1)}, u32[]{:S(2)}, u32[]{:S(2)}) collective-permute-start(f32[2,64,256]{2,1,0:T(8,128)S(1)} %pad_maximum_fusion.20), channel_id=1, source_target_pairs={{0,16},{1,17},{2,18},{3,19},{4,20},{5,21},{6,22},{7,23},{8,24},{9,... | collective-permute-start | bytes 393224 | tf_op jit(solution)/shard_map/while/body/eval_jaxpr/ppermute | solution.py:85
  252.4 3.8 collective-permute-done.4
  257.2 24.8 %eval_jaxpr.11 = (f32[64,1,256]{2,1,0:T(1,128)}, f32[64,1,256]{2,1,0:T(1,128)}) custom-call(s32[64]{0:T(128)S(1)} %get-tuple-element.682.rhs_slot.lhs_slot, s32[64]{0:T(128)S(1)} %get-tuple-element.681.lhs_slot.rhs_slot, bf16[64,256,64]{2,1,0:T(8,128)(2,1)} %get-tuple-element.688.lhs_ref, bf16[4,64,256]{2,1,0:T(8,128)(2,1)S(1)} %get-tuple-element.689.rhs_ref, ...), custom_call_target="tpu_custom_call" | custom-call | flops 536870912 | bytes 2359296 | tf_op jit(solution)/shard_map/while/body/eval_jaxpr/pallas_call | solution.py:51
  284.7 8.5 %collective-permute-start.5 = (f32[2,4,256]{2,1,0:T(4,128)S(1)}, f32[2,4,256]{2,1,0:T(4,128)S(1)}, u32[]{:S(2)}, u32[]{:S(2)}) collective-permute-start(f32[2,4,256]{2,1,0:T(4,128)S(1)} %pad_maximum_fusion.21), channel_id=1, source_target_pairs={{0,32},{32,0},{64,96},{96,64},{128,160},{160,128},{192,224},{224,1... | collective-permute-start | bytes 24584 | tf_op jit(solution)/shard_map/while/body/eval_jaxpr/ppermute | solution.py:85
  296.7 2.8 collective-permute-start.7
  301.5 17.3 %eval_jaxpr.10 = (f32[64,1,256]{2,1,0:T(1,128)}, f32[64,1,256]{2,1,0:T(1,128)}) custom-call(s32[64]{0:T(128)S(1)} %get-tuple-element.681.lhs_slot.rhs_slot, s32[64]{0:T(128)S(1)} %get-tuple-element.682.rhs_slot.lhs_slot, bf16[4,256,64]{2,1,0:T(8,128)(2,1)S(1)} %get-tuple-element.683.lhs_ref, bf16[64,64,256]{2,1,0:T(8,128)(2,1)S(1)} %get-tuple-element.684.rhs_ref, ...), custom_call_target="tpu_custom_call" | custom-call | flops 536870912 | bytes 2359296 | tf_op jit(solution)/shard_map/while/body/eval_jaxpr/pallas_call | solution.py:51
  322.7 3.7 collective-permute-start
  326.4 2.4 collective-permute-done
  328.8 3.9 collective-permute-start.1
  332.7 3.2 collective-permute-done.1
  336.1 3.8 collective-permute-done.2
  340.5 5.5 %collective-permute-done.3 = f32[2,64,256]{2,1,0:T(8,128)S(1)} collective-permute-done((f32[2,64,256]{2,1,0:T(8,128)S(1)}, f32[2,64,256]{2,1,0:T(8,128)S(1)}, u32[]{:S(2)}, u32[]{:S(2)}) %collective-permute-start.3) | collective-permute-done | bytes 131104 | tf_op jit(solution)/shard_map/while/body/eval_jaxpr/ppermute | solution.py:85
  346.1 3.2 collective-permute-start.4
  349.3 5.8 %collective-permute-done.4 = f32[2,64,256]{2,1,0:T(8,128)S(1)} collective-permute-done((f32[2,64,256]{2,1,0:T(8,128)S(1)}, f32[2,64,256]{2,1,0:T(8,128)S(1)}, u32[]{:S(2)}, u32[]{:S(2)}) %collective-permute-start.4) | collective-permute-done | bytes 131104 | tf_op jit(solution)/shard_map/while/body/eval_jaxpr/ppermute | solution.py:85
  356.1 24.7 %eval_jaxpr.11 = (f32[64,1,256]{2,1,0:T(1,128)}, f32[64,1,256]{2,1,0:T(1,128)}) custom-call(s32[64]{0:T(128)S(1)} %get-tuple-element.682.rhs_slot.lhs_slot, s32[64]{0:T(128)S(1)} %get-tuple-element.681.lhs_slot.rhs_slot, bf16[64,256,64]{2,1,0:T(8,128)(2,1)} %get-tuple-element.688.lhs_ref, bf16[4,64,256]{2,1,0:T(8,128)(2,1)S(1)} %get-tuple-element.689.rhs_ref, ...), custom_call_target="tpu_custom_call" | custom-call | flops 536870912 | bytes 2359296 | tf_op jit(solution)/shard_map/while/body/eval_jaxpr/pallas_call | solution.py:51
  383.6 10.3 %collective-permute-start.5 = (f32[2,4,256]{2,1,0:T(4,128)S(1)}, f32[2,4,256]{2,1,0:T(4,128)S(1)}, u32[]{:S(2)}, u32[]{:S(2)}) collective-permute-start(f32[2,4,256]{2,1,0:T(4,128)S(1)} %pad_maximum_fusion.21), channel_id=1, source_target_pairs={{0,32},{32,0},{64,96},{96,64},{128,160},{160,128},{192,224},{224,1... | collective-permute-start | bytes 24584 | tf_op jit(solution)/shard_map/while/body/eval_jaxpr/ppermute | solution.py:85
  397.4 2.8 collective-permute-start.7
  (237 shorter events, 69.5 us)
Async XLA Ops:
  0.6 7.0 %copy-start = (bf16[64,64,256]{2,1,0:T(8,128)(2,1)S(1)}, bf16[64,64,256]{2,1,0:T(8,128)(2,1)}, u32[]{:S(2)}) copy-start(bf16[64,64,256]{2,1,0:T(8,128)(2,1)} %param.5) | copy-start | bytes 6291460
  4.4 6.5 %copy-start.1 = (bf16[4,64,256]{2,1,0:T(8,128)(2,1)S(1)}, bf16[4,64,256]{2,1,0:T(8,128)(2,1)}, u32[]{:S(2)}) copy-start(bf16[4,64,256]{2,1,0:T(8,128)(2,1)} %param.6) | copy-start | bytes 393220
  32.9 4.6 %collective-permute-start = (f32[2,64,256]{2,1,0:T(8,128)S(1)}, f32[2,64,256]{2,1,0:T(8,128)S(1)}, u32[]{:S(2)}, u32[]{:S(2)}) collective-permute-start(f32[2,64,256]{2,1,0:T(8,128)S(1)} %pad_maximum_fusion.16), channel_id=1, source_target_pairs={{0,1},{1,0},{2,3},{3,2},{4,5},{5,4},{6,7},{7,6},{8,9},{9,8},{10,11... | collective-permute-start | bytes 393224 | tf_op jit(solution)/shard_map/while/body/eval_jaxpr/ppermute | solution.py:85
  37.5 6.1 %collective-permute-start.1 = (f32[2,64,256]{2,1,0:T(8,128)S(1)}, f32[2,64,256]{2,1,0:T(8,128)S(1)}, u32[]{:S(2)}, u32[]{:S(2)}) collective-permute-start(f32[2,64,256]{2,1,0:T(8,128)S(1)} %pad_maximum_fusion.17), channel_id=1, source_target_pairs={{0,2},{1,3},{2,0},{3,1},{4,6},{5,7},{6,4},{7,5},{8,10},{9,11},{10,... | collective-permute-start | bytes 393224 | tf_op jit(solution)/shard_map/while/body/eval_jaxpr/ppermute | solution.py:85
  43.7 4.1 %collective-permute-start.2 = (f32[2,64,256]{2,1,0:T(8,128)S(1)}, f32[2,64,256]{2,1,0:T(8,128)S(1)}, u32[]{:S(2)}, u32[]{:S(2)}) collective-permute-start(f32[2,64,256]{2,1,0:T(8,128)S(1)} %pad_maximum_fusion.18), channel_id=1, source_target_pairs={{0,4},{1,5},{2,6},{3,7},{4,0},{5,1},{6,2},{7,3},{8,12},{9,13},{10,... | collective-permute-start | bytes 393224 | tf_op jit(solution)/shard_map/while/body/eval_jaxpr/ppermute | solution.py:85
  47.9 5.7 %collective-permute-start.3 = (f32[2,64,256]{2,1,0:T(8,128)S(1)}, f32[2,64,256]{2,1,0:T(8,128)S(1)}, u32[]{:S(2)}, u32[]{:S(2)}) collective-permute-start(f32[2,64,256]{2,1,0:T(8,128)S(1)} %pad_maximum_fusion.19), channel_id=1, source_target_pairs={{0,8},{1,9},{2,10},{3,11},{4,12},{5,13},{6,14},{7,15},{8,0},{9,1},... | collective-permute-start | bytes 393224 | tf_op jit(solution)/shard_map/while/body/eval_jaxpr/ppermute | solution.py:85
  53.8 10.4 %collective-permute-start.4 = (f32[2,64,256]{2,1,0:T(8,128)S(1)}, f32[2,64,256]{2,1,0:T(8,128)S(1)}, u32[]{:S(2)}, u32[]{:S(2)}) collective-permute-start(f32[2,64,256]{2,1,0:T(8,128)S(1)} %pad_maximum_fusion.20), channel_id=1, source_target_pairs={{0,16},{1,17},{2,18},{3,19},{4,20},{5,21},{6,22},{7,23},{8,24},{9,... | collective-permute-start | bytes 393224 | tf_op jit(solution)/shard_map/while/body/eval_jaxpr/ppermute | solution.py:85
  92.7 7.4 %collective-permute-start.5 = (f32[2,4,256]{2,1,0:T(4,128)S(1)}, f32[2,4,256]{2,1,0:T(4,128)S(1)}, u32[]{:S(2)}, u32[]{:S(2)}) collective-permute-start(f32[2,4,256]{2,1,0:T(4,128)S(1)} %pad_maximum_fusion.21), channel_id=1, source_target_pairs={{0,32},{32,0},{64,96},{96,64},{128,160},{160,128},{192,224},{224,1... | collective-permute-start | bytes 24584 | tf_op jit(solution)/shard_map/while/body/eval_jaxpr/ppermute | solution.py:85
  100.1 2.6 collective-permute-start.6
  102.7 4.1 %collective-permute-start.7 = (f32[2,4,256]{2,1,0:T(4,128)S(1)}, f32[2,4,256]{2,1,0:T(4,128)S(1)}, u32[]{:S(2)}, u32[]{:S(2)}) collective-permute-start(f32[2,4,256]{2,1,0:T(4,128)S(1)} %pad_maximum_fusion.23), channel_id=1, source_target_pairs={{0,128},{32,160},{64,192},{96,224},{128,0},{160,32},{192,64},{224,... | collective-permute-start | bytes 24584 | tf_op jit(solution)/shard_map/while/body/eval_jaxpr/ppermute | solution.py:85
  128.7 3.9 collective-permute-start
  132.7 6.8 %collective-permute-start.1 = (f32[2,64,256]{2,1,0:T(8,128)S(1)}, f32[2,64,256]{2,1,0:T(8,128)S(1)}, u32[]{:S(2)}, u32[]{:S(2)}) collective-permute-start(f32[2,64,256]{2,1,0:T(8,128)S(1)} %pad_maximum_fusion.17), channel_id=1, source_target_pairs={{0,2},{1,3},{2,0},{3,1},{4,6},{5,7},{6,4},{7,5},{8,10},{9,11},{10,... | collective-permute-start | bytes 393224 | tf_op jit(solution)/shard_map/while/body/eval_jaxpr/ppermute | solution.py:85
  139.5 3.9 collective-permute-start.2
  143.5 6.1 %collective-permute-start.3 = (f32[2,64,256]{2,1,0:T(8,128)S(1)}, f32[2,64,256]{2,1,0:T(8,128)S(1)}, u32[]{:S(2)}, u32[]{:S(2)}) collective-permute-start(f32[2,64,256]{2,1,0:T(8,128)S(1)} %pad_maximum_fusion.19), channel_id=1, source_target_pairs={{0,8},{1,9},{2,10},{3,11},{4,12},{5,13},{6,14},{7,15},{8,0},{9,1},... | collective-permute-start | bytes 393224 | tf_op jit(solution)/shard_map/while/body/eval_jaxpr/ppermute | solution.py:85
  149.7 9.6 %collective-permute-start.4 = (f32[2,64,256]{2,1,0:T(8,128)S(1)}, f32[2,64,256]{2,1,0:T(8,128)S(1)}, u32[]{:S(2)}, u32[]{:S(2)}) collective-permute-start(f32[2,64,256]{2,1,0:T(8,128)S(1)} %pad_maximum_fusion.20), channel_id=1, source_target_pairs={{0,16},{1,17},{2,18},{3,19},{4,20},{5,21},{6,22},{7,23},{8,24},{9,... | collective-permute-start | bytes 393224 | tf_op jit(solution)/shard_map/while/body/eval_jaxpr/ppermute | solution.py:85
  187.7 9.3 %collective-permute-start.5 = (f32[2,4,256]{2,1,0:T(4,128)S(1)}, f32[2,4,256]{2,1,0:T(4,128)S(1)}, u32[]{:S(2)}, u32[]{:S(2)}) collective-permute-start(f32[2,4,256]{2,1,0:T(4,128)S(1)} %pad_maximum_fusion.21), channel_id=1, source_target_pairs={{0,32},{32,0},{64,96},{96,64},{128,160},{160,128},{192,224},{224,1... | collective-permute-start | bytes 24584 | tf_op jit(solution)/shard_map/while/body/eval_jaxpr/ppermute | solution.py:85
  197.1 2.6 collective-permute-start.6
  199.7 4.1 %collective-permute-start.7 = (f32[2,4,256]{2,1,0:T(4,128)S(1)}, f32[2,4,256]{2,1,0:T(4,128)S(1)}, u32[]{:S(2)}, u32[]{:S(2)}) collective-permute-start(f32[2,4,256]{2,1,0:T(4,128)S(1)} %pad_maximum_fusion.23), channel_id=1, source_target_pairs={{0,128},{32,160},{64,192},{96,224},{128,0},{160,32},{192,64},{224,... | collective-permute-start | bytes 24584 | tf_op jit(solution)/shard_map/while/body/eval_jaxpr/ppermute | solution.py:85
  225.7 4.1 %collective-permute-start = (f32[2,64,256]{2,1,0:T(8,128)S(1)}, f32[2,64,256]{2,1,0:T(8,128)S(1)}, u32[]{:S(2)}, u32[]{:S(2)}) collective-permute-start(f32[2,64,256]{2,1,0:T(8,128)S(1)} %pad_maximum_fusion.16), channel_id=1, source_target_pairs={{0,1},{1,0},{2,3},{3,2},{4,5},{5,4},{6,7},{7,6},{8,9},{9,8},{10,11... | collective-permute-start | bytes 393224 | tf_op jit(solution)/shard_map/while/body/eval_jaxpr/ppermute | solution.py:85
  229.9 6.6 %collective-permute-start.1 = (f32[2,64,256]{2,1,0:T(8,128)S(1)}, f32[2,64,256]{2,1,0:T(8,128)S(1)}, u32[]{:S(2)}, u32[]{:S(2)}) collective-permute-start(f32[2,64,256]{2,1,0:T(8,128)S(1)} %pad_maximum_fusion.17), channel_id=1, source_target_pairs={{0,2},{1,3},{2,0},{3,1},{4,6},{5,7},{6,4},{7,5},{8,10},{9,11},{10,... | collective-permute-start | bytes 393224 | tf_op jit(solution)/shard_map/while/body/eval_jaxpr/ppermute | solution.py:85
  236.6 3.9 collective-permute-start.2
  240.6 6.1 %collective-permute-start.3 = (f32[2,64,256]{2,1,0:T(8,128)S(1)}, f32[2,64,256]{2,1,0:T(8,128)S(1)}, u32[]{:S(2)}, u32[]{:S(2)}) collective-permute-start(f32[2,64,256]{2,1,0:T(8,128)S(1)} %pad_maximum_fusion.19), channel_id=1, source_target_pairs={{0,8},{1,9},{2,10},{3,11},{4,12},{5,13},{6,14},{7,15},{8,0},{9,1},... | collective-permute-start | bytes 393224 | tf_op jit(solution)/shard_map/while/body/eval_jaxpr/ppermute | solution.py:85
  246.8 9.4 %collective-permute-start.4 = (f32[2,64,256]{2,1,0:T(8,128)S(1)}, f32[2,64,256]{2,1,0:T(8,128)S(1)}, u32[]{:S(2)}, u32[]{:S(2)}) collective-permute-start(f32[2,64,256]{2,1,0:T(8,128)S(1)} %pad_maximum_fusion.20), channel_id=1, source_target_pairs={{0,16},{1,17},{2,18},{3,19},{4,20},{5,21},{6,22},{7,23},{8,24},{9,... | collective-permute-start | bytes 393224 | tf_op jit(solution)/shard_map/while/body/eval_jaxpr/ppermute | solution.py:85
  284.7 9.3 %collective-permute-start.5 = (f32[2,4,256]{2,1,0:T(4,128)S(1)}, f32[2,4,256]{2,1,0:T(4,128)S(1)}, u32[]{:S(2)}, u32[]{:S(2)}) collective-permute-start(f32[2,4,256]{2,1,0:T(4,128)S(1)} %pad_maximum_fusion.21), channel_id=1, source_target_pairs={{0,32},{32,0},{64,96},{96,64},{128,160},{160,128},{192,224},{224,1... | collective-permute-start | bytes 24584 | tf_op jit(solution)/shard_map/while/body/eval_jaxpr/ppermute | solution.py:85
  294.1 2.6 collective-permute-start.6
  296.7 4.1 %collective-permute-start.7 = (f32[2,4,256]{2,1,0:T(4,128)S(1)}, f32[2,4,256]{2,1,0:T(4,128)S(1)}, u32[]{:S(2)}, u32[]{:S(2)}) collective-permute-start(f32[2,4,256]{2,1,0:T(4,128)S(1)} %pad_maximum_fusion.23), channel_id=1, source_target_pairs={{0,128},{32,160},{64,192},{96,224},{128,0},{160,32},{192,64},{224,... | collective-permute-start | bytes 24584 | tf_op jit(solution)/shard_map/while/body/eval_jaxpr/ppermute | solution.py:85
  322.7 6.0 %collective-permute-start = (f32[2,64,256]{2,1,0:T(8,128)S(1)}, f32[2,64,256]{2,1,0:T(8,128)S(1)}, u32[]{:S(2)}, u32[]{:S(2)}) collective-permute-start(f32[2,64,256]{2,1,0:T(8,128)S(1)} %pad_maximum_fusion.16), channel_id=1, source_target_pairs={{0,1},{1,0},{2,3},{3,2},{4,5},{5,4},{6,7},{7,6},{8,9},{9,8},{10,11... | collective-permute-start | bytes 393224 | tf_op jit(solution)/shard_map/while/body/eval_jaxpr/ppermute | solution.py:85
  328.8 7.1 %collective-permute-start.1 = (f32[2,64,256]{2,1,0:T(8,128)S(1)}, f32[2,64,256]{2,1,0:T(8,128)S(1)}, u32[]{:S(2)}, u32[]{:S(2)}) collective-permute-start(f32[2,64,256]{2,1,0:T(8,128)S(1)} %pad_maximum_fusion.17), channel_id=1, source_target_pairs={{0,2},{1,3},{2,0},{3,1},{4,6},{5,7},{6,4},{7,5},{8,10},{9,11},{10,... | collective-permute-start | bytes 393224 | tf_op jit(solution)/shard_map/while/body/eval_jaxpr/ppermute | solution.py:85
  336.0 3.9 collective-permute-start.2
  340.0 6.1 %collective-permute-start.3 = (f32[2,64,256]{2,1,0:T(8,128)S(1)}, f32[2,64,256]{2,1,0:T(8,128)S(1)}, u32[]{:S(2)}, u32[]{:S(2)}) collective-permute-start(f32[2,64,256]{2,1,0:T(8,128)S(1)} %pad_maximum_fusion.19), channel_id=1, source_target_pairs={{0,8},{1,9},{2,10},{3,11},{4,12},{5,13},{6,14},{7,15},{8,0},{9,1},... | collective-permute-start | bytes 393224 | tf_op jit(solution)/shard_map/while/body/eval_jaxpr/ppermute | solution.py:85
  346.1 9.0 %collective-permute-start.4 = (f32[2,64,256]{2,1,0:T(8,128)S(1)}, f32[2,64,256]{2,1,0:T(8,128)S(1)}, u32[]{:S(2)}, u32[]{:S(2)}) collective-permute-start(f32[2,64,256]{2,1,0:T(8,128)S(1)} %pad_maximum_fusion.20), channel_id=1, source_target_pairs={{0,16},{1,17},{2,18},{3,19},{4,20},{5,21},{6,22},{7,23},{8,24},{9,... | collective-permute-start | bytes 393224 | tf_op jit(solution)/shard_map/while/body/eval_jaxpr/ppermute | solution.py:85
  383.6 11.1 %collective-permute-start.5 = (f32[2,4,256]{2,1,0:T(4,128)S(1)}, f32[2,4,256]{2,1,0:T(4,128)S(1)}, u32[]{:S(2)}, u32[]{:S(2)}) collective-permute-start(f32[2,4,256]{2,1,0:T(4,128)S(1)} %pad_maximum_fusion.21), channel_id=1, source_target_pairs={{0,32},{32,0},{64,96},{96,64},{128,160},{160,128},{192,224},{224,1... | collective-permute-start | bytes 24584 | tf_op jit(solution)/shard_map/while/body/eval_jaxpr/ppermute | solution.py:85
  394.8 2.6 collective-permute-start.6
  397.4 4.1 %collective-permute-start.7 = (f32[2,4,256]{2,1,0:T(4,128)S(1)}, f32[2,4,256]{2,1,0:T(4,128)S(1)}, u32[]{:S(2)}, u32[]{:S(2)}) collective-permute-start(f32[2,4,256]{2,1,0:T(4,128)S(1)} %pad_maximum_fusion.23), channel_id=1, source_target_pairs={{0,128},{32,160},{64,192},{96,224},{128,0},{160,32},{192,64},{224,... | collective-permute-start | bytes 24584 | tf_op jit(solution)/shard_map/while/body/eval_jaxpr/ppermute | solution.py:85
  401.5 0.6 copy-start.2
